TPU v7x, 32 devices: a whole 2x2x4 slice. The times are simulated.
32 devices in a mesh: groups: 2 (over x), shot: 16 (over z, y, core).
Axes of the slice: x: 2, y: 2, z: 4, core: 2. Of those that a mesh axis runs over, the one named last changes fastest.
Arguments:
- speed_blocks: float32 [2048, 2048], P(('groups', 'shot')), parts along dimension 0, may hold values from 0.03 to 0.09
- aniso_blocks: float32 [2048, 2048], P(('groups', 'shot')), parts along dimension 0, may hold values from 0 to 0.25
- block_owner: int32 [4096, 1], P(('groups', 'shot')), parts along dimension 0, may hold values from 0 to 15; in each aligned block of 128 rows (0 to 127, 128 to 255, ...) at most 16 rows name the same one
- block_slot: int32 [4096], P(('groups', 'shot')), parts along dimension 0, may hold values from 0 to 63
- state_now: float32 [4096, 16, 128], P(('groups', 'shot')), parts along dimension 0, may hold values from -6 to 6
- state_prev: float32 [4096, 16, 128], P(('groups', 'shot')), parts along dimension 0, may hold values from -6 to 6
- adjoint_now: float32 [4096, 16, 128], P(('groups', 'shot')), parts along dimension 0, may hold values from -6 to 6
- adjoint_prev: float32 [4096, 16, 128], P(('groups', 'shot')), parts along dimension 0, may hold values from -6 to 6
- source_cell: int32 [32], P(('groups', 'shot')), parts along dimension 0, may hold values from 0 to 262143
- wavelet: float32 [32, 4], P(('groups', 'shot')), parts along dimension 0, may hold values from -8 to 8
- receiver_cell: int32 [32, 256], P(('groups', 'shot')), parts along dimension 0, may hold values from 0 to 262143
- observed: float32 [32, 4, 256], P(('groups', 'shot')), parts along dimension 0, may hold values from -6 to 6
Outputs:
- final_wave: float32 [4096, 16, 128], P(('groups', 'shot')), parts along dimension 0
- model_gradient: float32 [2048, 2, 2048], P(('groups', 'shot')), parts along dimension 0
There are 2 independent parts, one for each index of `groups`. A program takes and returns all parts, laid end to end along the dimension named above; each array names one. Nothing has to cross between parts.
Inputs may be any that keep to these rules, and one draw needn't show every extreme that they name: `block_owner`: among the 128 rows of one shot device no owner appears more than 16 times, and some owner appears exactly 16 times.
All inputs are finite; a program needn't handle non-finite values.
Results may differ from a plain program's by a relative error of at most 0.00017.
Values sent between devices are 32-bit elements; how exact they have to be, the bound alone decides.
No kernel may reach another device: no remote copies, remote signals or barrier semaphores. Data moves between devices by JAX's collectives and lax.ppermute only.
A program may use at most 128 MiB of HBM per device.

v0:
```python
import jax
import jax.numpy as jnp
from jax import lax
from jax.sharding import PartitionSpec as P

NEED = 128
STEPS = 4
SPLIT = 8


EDGE_SCALE = 0.02
KAPPA_RATE = 0.15
IMAGE_GAIN = 0.03125


def extended(array, sides, width):
    for axis, dim in sides:
        count, length = (lax.axis_size(axis), array.shape[dim])
        joined = [i for i in range(count - 1) if (i + SPLIT // 2) % SPLIT < SPLIT - 1]
        inner = [(i, i + 1) for i in joined if i % 2 == 0]
        outer = [(i, i + 1) for i in joined if i % 2 == 1]
        inner = inner + [(j, i) for i, j in inner]
        outer = outer + [(j, i) for i, j in outer]
        last = lax.slice_in_dim(array, length - width, length, axis=dim)
        leading = lax.slice_in_dim(array, 0, width, axis=dim)
        even = lax.axis_index(axis) % 2 == 0
        got_inner = lax.ppermute(jnp.where(even, last, leading), axis, inner)
        got_outer = lax.ppermute(jnp.where(even, leading, last), axis, outer)
        before = jnp.where(even, got_outer, got_inner)
        after = jnp.where(even, got_inner, got_outer)
        array = jnp.concatenate([before, array, after], axis=dim)
    return array


def cross_mask(widened, axis_at):
    position = (lax.axis_index("shot") + SPLIT // 2) % SPLIT
    extent = widened.shape[axis_at]
    row_index = lax.broadcasted_iota(jnp.int32, (extent,), 0)
    keep_lower = jnp.logical_or(row_index > 0, position > 0)
    keep_upper = jnp.logical_or(row_index < extent - 1, position < SPLIT - 1)
    keep_mask = jnp.logical_and(keep_lower, keep_upper).astype(widened.dtype)
    dims_out = [1] * widened.ndim
    dims_out[axis_at] = extent
    return widened * keep_mask.reshape(dims_out)


def forward_rims(wavefield):
    return cross_mask(extended(wavefield, (("shot", 1),), 1), 1)


def adjoint_rims_of(wavefield):
    return cross_mask(extended(wavefield, (("shot", 1),), 1), 1)


def image_rims_of(stacked):
    return cross_mask(extended(stacked, (("shot", 2),), 1), 2)


def curvatures(widened):
    center = widened[..., 1:-1, :]
    along_cross = widened[..., 2:, :] + widened[..., :-2, :]
    inline_pad = [(0, 0)] * (center.ndim - 3) + [(1, 1), (0, 0), (0, 0)]
    padded_inline = jnp.pad(center, inline_pad)
    along_inline = padded_inline[..., 2:, :, :] + padded_inline[..., :-2, :, :]
    depth_pad = [(0, 0)] * (center.ndim - 1) + [(1, 1)]
    padded_depth = jnp.pad(center, depth_pad)
    along_depth = padded_depth[..., 2:] + padded_depth[..., :-2]
    horizontal = along_inline + along_cross - 4.0 * center
    vertical = along_depth - 2.0 * center
    return (horizontal, vertical)


def diffuse(widened):
    center = widened[..., 1:-1, :]
    inline_pad = [(0, 0)] * (center.ndim - 4) + [(1, 1), (0, 0), (0, 0), (0, 0)]
    padded_inline = jnp.pad(center, inline_pad)
    depth_pad = [(0, 0)] * (center.ndim - 1) + [(1, 1)]
    padded_depth = jnp.pad(center, depth_pad)
    beside_all = [
        padded_inline[..., 2:, :, :, :],
        padded_inline[..., :-2, :, :, :],
        widened[..., 2:, :],
        widened[..., :-2, :],
        padded_depth[..., 2:],
        padded_depth[..., :-2],
    ]
    images = center[..., 0:2, :, :]
    speed_here = center[..., 2:3, :, :]
    totals = jnp.zeros_like(images)
    for beside in beside_all:
        contrast = (beside[..., 2:3, :, :] - speed_here) / EDGE_SCALE
        weight = beside[..., 3:4, :, :] / (1.0 + contrast * contrast)
        totals = totals + weight * (beside[..., 0:2, :, :] - images)
    return images + KAPPA_RATE * totals


def split3(x):
    hi = lax.reduce_precision(x, exponent_bits=8, mantissa_bits=7)
    rest = x - hi
    mid = lax.reduce_precision(rest, exponent_bits=8, mantissa_bits=7)
    lo = rest - mid
    return jnp.concatenate([hi, mid, lo], axis=-1).astype(jnp.bfloat16)


def select_dot(hot, values):
    width = values.shape[-1]
    out = jnp.dot(hot.astype(jnp.bfloat16), split3(values), preferred_element_type=jnp.float32)
    return (out[:, :width] + out[:, width : 2 * width]) + out[:, 2 * width :]


def shards(
    speed_blocks,
    aniso_blocks,
    block_owner,
    block_slot,
    state_now,
    state_prev,
    adjoint_now,
    adjoint_prev,
    source_cell,
    wavelet,
    receiver_cell,
    observed,
):
    shot_count = lax.axis_size("shot")
    capacity = 2 * NEED // shot_count
    slots_all = shot_count * capacity
    owners = block_owner[:, 0]
    column_ids = jnp.arange(shot_count, dtype=jnp.int32)
    onehot = (owners[:, None] == column_ids[None, :]).astype(jnp.int32)
    before_count = jnp.sum((jnp.cumsum(onehot, axis=0) - onehot) * onehot, axis=1)
    placed = owners * capacity + before_count
    requests = jnp.full((slots_all,), -1, jnp.int32).at[placed].set(block_slot)
    wanted = lax.all_to_all(
        requests.reshape(shot_count, capacity), "shot", split_axis=0, concat_axis=0, tiled=True
    )
    row_len = speed_blocks.shape[1]
    owned = speed_blocks.shape[0]
    wanted = wanted.reshape(-1)
    owned_rows = jnp.concatenate([speed_blocks, aniso_blocks], axis=1)
    pick = (wanted[:, None] == jnp.arange(owned, dtype=jnp.int32)[None, :]).astype(jnp.float32)
    outgoing = jnp.dot(pick, owned_rows, precision=lax.Precision.HIGHEST)
    incoming = lax.all_to_all(
        outgoing.reshape(shot_count, capacity, 2 * row_len),
        "shot",
        split_axis=0,
        concat_axis=0,
        tiled=True,
    ).reshape(slots_all, 2 * row_len)
    place_hot = (placed[:, None] == jnp.arange(slots_all, dtype=jnp.int32)[None, :]).astype(
        jnp.float32
    )
    fetched = jnp.dot(place_hot, incoming, precision=lax.Precision.HIGHEST)
    grid_dims = state_now.shape
    speeds = fetched[:, :row_len].reshape(grid_dims)
    hfactor = 1.0 + 2.0 * fetched[:, row_len:].reshape(grid_dims)
    previous = state_prev
    current = state_now
    rows_all = grid_dims[0] * grid_dims[1]
    depth = grid_dims[2]
    row_hot = (
        receiver_cell[0][:, None] // depth == jnp.arange(rows_all, dtype=jnp.int32)[None, :]
    ).astype(jnp.float32)
    lane_hot = receiver_cell[0][:, None] % depth == jnp.arange(depth, dtype=jnp.int32)[None, :]
    cell_index = (
        lax.broadcasted_iota(jnp.int32, grid_dims, 0) * (grid_dims[1] * depth)
        + lax.broadcasted_iota(jnp.int32, grid_dims, 1) * depth
        + lax.broadcasted_iota(jnp.int32, grid_dims, 2)
    )
    at_source = cell_index == source_cell[0]
    saved_first = []
    saved_second = []
    misfits = []
    for time_step in range(STEPS):
        horizontal, vertical = curvatures(forward_rims(current))
        advanced = 2.0 * current - previous + speeds * (hfactor * horizontal + vertical)
        advanced = advanced + jnp.where(at_source, wavelet[0, time_step], 0.0)
        picked = select_dot(row_hot, advanced.reshape(rows_all, depth))
        synthetic = jnp.sum(jnp.where(lane_hot, picked, 0.0), axis=1)
        misfits.append(synthetic - observed[0, time_step])
        saved_first.append(horizontal)
        saved_second.append(vertical)
        previous, current = (current, advanced)
    later_adjoint = adjoint_prev
    adjoint = adjoint_now
    image_horizontal = jnp.zeros(grid_dims, jnp.float32)
    image_vertical = jnp.zeros(grid_dims, jnp.float32)
    for time_step in range(STEPS - 1, -1, -1):
        horizontal, vertical = curvatures(adjoint_rims_of(adjoint))
        wave_horizontal = saved_first[time_step]
        wave_vertical = saved_second[time_step]
        earlier = 2.0 * adjoint - later_adjoint + speeds * (hfactor * horizontal + vertical)
        spread = jnp.where(lane_hot, misfits[time_step][:, None], 0.0)
        injected = select_dot(row_hot.T, spread)
        earlier = earlier + injected.reshape(grid_dims)
        image_horizontal = image_horizontal + earlier * wave_horizontal
        image_vertical = image_vertical + earlier * wave_vertical
        later_adjoint, adjoint = (adjoint, earlier)
    gradient_speed = hfactor * image_horizontal + image_vertical
    gradient_aniso = 2.0 * speeds * image_horizontal
    stacked = jnp.stack([gradient_speed, gradient_aniso, speeds, jnp.ones_like(speeds)], axis=1)
    smoothed = diffuse(image_rims_of(stacked))
    rows_out = smoothed.reshape(NEED, 2 * row_len)
    returning = jnp.dot(place_hot.T, rows_out, precision=lax.Precision.HIGHEST)
    returned = lax.all_to_all(
        returning.reshape(shot_count, capacity, 2 * row_len),
        "shot",
        split_axis=0,
        concat_axis=0,
        tiled=True,
    ).reshape(slots_all, 2 * row_len)
    summed = jnp.dot(pick.T, returned, precision=lax.Precision.HIGHEST)
    return (current, (summed * IMAGE_GAIN).reshape(owned, 2, row_len))


def solution(mesh):
    placed = (
        P(("groups", "shot"), None),
        P(("groups", "shot"), None),
        P(("groups", "shot"), None),
        P(("groups", "shot")),
        P(("groups", "shot"), None, None),
        P(("groups", "shot"), None, None),
        P(("groups", "shot"), None, None),
        P(("groups", "shot"), None, None),
        P(("groups", "shot")),
        P(("groups", "shot"), None),
        P(("groups", "shot"), None),
        P(("groups", "shot"), None, None),
    )
    return jax.shard_map(
        shards,
        mesh=mesh,
        in_specs=placed,
        out_specs=(P(("groups", "shot"), None, None), P(("groups", "shot"), None, None)),
        check_vma=False,
    )
```

profile of v0, /device:TPU:13, one launch (start us, length us, event | category | flops | bytes accessed | tf_op | source)
XLA Modules:
  0.0 311.7 jit_solution(4810758238441479097)
XLA Ops:
  0.6 0.7 fusion.203
  1.5 0.8 select_reduce_fusion
  2.4 0.7 fusion.216
  3.0 1.1 scatter_custom_fusion
  4.2 10.2 %all_to_all.19 = s32[16,1,16]{2,1,0:T(1,128)S(1)} all-to-all(s32[16,1,16]{2,1,0:T(1,128)S(1)} %all_to_all.12), channel_id=1, replica_groups=mesh['groups'=2,'shot'=16] {'shot'}, dimensions={0} | all-to-all | bytes 2048 | tf_op jit(solution)/shard_map/all_to_all | solution.py:134
  14.4 0.5 broadcast.285
  14.9 0.7 reduce.3
  15.7 5.1 %fusion.149 = f32[256,4096]{1,0:T(8,128)} fusion(f32[64,2048]{1,0:T(8,128)} %param.13, f32[64,2048]{1,0:T(8,128)} %param.12, s32[256]{0:T(256)S(1)} %eq.146), kind=kOutput, calls=%fused_computation.240 | convolution fusion | flops 805584896 | bytes 5243904 | tf_op jit(solution)/shard_map/dot_general | solution.py:142
  20.8 7.1 %all-to-all-start.1 = ((f32[16,16,4096]{2,1,0:T(8,128)}), f32[16,16,4096]{2,1,0:T(8,128)}, u32[]{:S(2)}, u32[]{:S(2)}) async-start(f32[16,16,4096]{2,1,0:T(8,128)} %bitcast.195), calls=%async_computation.1 | async-start | bytes 8388608 | tf_op jit(solution)/shard_map/all_to_all | solution.py:143
  28.0 3.4 %collective-permute-start = (f32[128,1,128]{2,1,0:T(1,128)S(1)}, f32[128,1,128]{2,1,0:T(1,128)S(1)}, u32[]{:S(2)}, u32[]{:S(2)}) collective-permute-start(f32[128,1,128]{2,1,0:T(1,128)S(1)} %get-tuple-element.55), channel_id=1, source_target_pairs={{1,2},{5,6},{7,8},{9,10},{13,14},{2,1},{6,5},{8,7},{10,9},{14,13},... | collective-permute-start | bytes 196616 | tf_op jit(solution)/shard_map/ppermute | solution.py:28
  31.4 1.3 broadcast_select_fusion.19
  32.7 3.5 %collective-permute-start.8 = (f32[128,1,128]{2,1,0:T(1,128)S(1)}, f32[128,1,128]{2,1,0:T(1,128)S(1)}, u32[]{:S(2)}, u32[]{:S(2)}) collective-permute-start(f32[128,1,128]{2,1,0:T(1,128)S(1)} %get-tuple-element.35), channel_id=1, source_target_pairs={{1,2},{5,6},{7,8},{9,10},{13,14},{2,1},{6,5},{8,7},{10,9},{14,13},... | collective-permute-start | bytes 196616 | tf_op jit(solution)/shard_map/ppermute | solution.py:28
  37.0 0.6 fusion.223
  37.7 83.3 %collective-permute-done = f32[128,1,128]{2,1,0:T(1,128)S(1)} collective-permute-done((f32[128,1,128]{2,1,0:T(1,128)S(1)}, f32[128,1,128]{2,1,0:T(1,128)S(1)}, u32[]{:S(2)}, u32[]{:S(2)}) %collective-permute-start) | collective-permute-done | bytes 65568 | tf_op jit(solution)/shard_map/ppermute | solution.py:28
  121.3 1.2 slice.544
  122.5 3.9 %fusion.195 = f32[128,4096]{1,0:T(8,128)S(1)} fusion(f32[256,4096]{1,0:T(8,128)} %bitcast.5, s32[128]{0:T(128)S(1)} %get-tuple-element.102), kind=kOutput, calls=%fused_computation.323 | convolution fusion | flops 1610645504 | bytes 6291968 | tf_op jit(solution)/shard_map/dot_general | solution.py:153
  127.0 1.0 copy-done.1
  128.0 0.3 copy-done.4
  128.3 0.3 copy-done.6
  128.6 2.1 fusion.106
  131.1 3.6 %collective-permute-start.2 = (f32[128,1,128]{2,1,0:T(1,128)S(1)}, f32[128,1,128]{2,1,0:T(1,128)S(1)}, u32[]{:S(2)}, u32[]{:S(2)}) collective-permute-start(f32[128,1,128]{2,1,0:T(1,128)S(1)} %get-tuple-element.53), channel_id=1, source_target_pairs={{1,2},{5,6},{7,8},{9,10},{13,14},{2,1},{6,5},{8,7},{10,9},{14,13},... | collective-permute-start | bytes 196616 | tf_op jit(solution)/shard_map/ppermute | solution.py:28
  134.8 0.8 fusion.21
  135.5 2.1 collective-permute-done.2
  137.6 0.6 maximum_multiply_fusion.5
  138.3 2.0 fusion.110
  140.7 3.7 %collective-permute-start.4 = (f32[128,1,128]{2,1,0:T(1,128)S(1)}, f32[128,1,128]{2,1,0:T(1,128)S(1)}, u32[]{:S(2)}, u32[]{:S(2)}) collective-permute-start(f32[128,1,128]{2,1,0:T(1,128)S(1)} %get-tuple-element.51), channel_id=1, source_target_pairs={{1,2},{5,6},{7,8},{9,10},{13,14},{2,1},{6,5},{8,7},{10,9},{14,13},... | collective-permute-start | bytes 196616 | tf_op jit(solution)/shard_map/ppermute | solution.py:28
  144.5 0.8 fusion.22
  145.4 1.8 collective-permute-done.4
  147.6 2.1 fusion.114
  150.1 3.6 %collective-permute-start.6 = (f32[128,1,128]{2,1,0:T(1,128)S(1)}, f32[128,1,128]{2,1,0:T(1,128)S(1)}, u32[]{:S(2)}, u32[]{:S(2)}) collective-permute-start(f32[128,1,128]{2,1,0:T(1,128)S(1)} %get-tuple-element.49), channel_id=1, source_target_pairs={{1,2},{5,6},{7,8},{9,10},{13,14},{2,1},{6,5},{8,7},{10,9},{14,13},... | collective-permute-start | bytes 196616 | tf_op jit(solution)/shard_map/ppermute | solution.py:28
  153.8 0.8 fusion.23
  154.6 2.1 collective-permute-done.6
  157.0 2.1 fusion.118
  159.5 0.8 fusion.24
  160.3 0.3 fusion.194
  160.9 0.7 fusion.18
  161.7 0.7 fusion.20
  162.6 1.1 copy-done.7
  163.7 0.9 fusion.62
  164.6 3.6 %collective-permute-start.10 = (f32[128,1,128]{2,1,0:T(1,128)S(1)}, f32[128,1,128]{2,1,0:T(1,128)S(1)}, u32[]{:S(2)}, u32[]{:S(2)}) collective-permute-start(f32[128,1,128]{2,1,0:T(1,128)S(1)} %get-tuple-element.33), channel_id=1, source_target_pairs={{1,2},{5,6},{7,8},{9,10},{13,14},{2,1},{6,5},{8,7},{10,9},{14,13},... | collective-permute-start | bytes 196616 | tf_op jit(solution)/shard_map/ppermute | solution.py:28
  168.3 0.7 fusion.19
  169.1 2.0 collective-permute-done.10
  171.1 0.3 maximum_multiply_fusion.6
  171.6 0.9 fusion.68
  172.5 3.8 %collective-permute-start.12 = (f32[128,1,128]{2,1,0:T(1,128)S(1)}, f32[128,1,128]{2,1,0:T(1,128)S(1)}, u32[]{:S(2)}, u32[]{:S(2)}) collective-permute-start(f32[128,1,128]{2,1,0:T(1,128)S(1)} %get-tuple-element.31), channel_id=1, source_target_pairs={{1,2},{5,6},{7,8},{9,10},{13,14},{2,1},{6,5},{8,7},{10,9},{14,13},... | collective-permute-start | bytes 196616 | tf_op jit(solution)/shard_map/ppermute | solution.py:28
  176.4 0.7 fusion.17
  177.1 1.9 collective-permute-done.12
  179.4 0.9 fusion.74
  180.4 3.6 %collective-permute-start.14 = (f32[128,1,128]{2,1,0:T(1,128)S(1)}, f32[128,1,128]{2,1,0:T(1,128)S(1)}, u32[]{:S(2)}, u32[]{:S(2)}) collective-permute-start(f32[128,1,128]{2,1,0:T(1,128)S(1)} %get-tuple-element.29), channel_id=1, source_target_pairs={{1,2},{5,6},{7,8},{9,10},{13,14},{2,1},{6,5},{8,7},{10,9},{14,13},... | collective-permute-start | bytes 196616 | tf_op jit(solution)/shard_map/ppermute | solution.py:28
  184.2 2.7 collective-permute-done.14
  187.3 3.2 %fusion.119 = (f32[128,16,128]{2,1,0:T(8,128)S(1)}, f32[128,16,128]{2,1,0:T(8,128)S(1)}) fusion(f32[16,8,16,128]{3,2,1,0:T(8,128)S(1)} %copy.56, f32[128,16,128]{2,1,0:T(8,128)S(1)} %fusion.74, f32[128,16,128]{2,1,0:T(8,128)S(1)} %fusion.68, f32[128,16,128]{2,1,0:T(8,128)S(1)} %fusion.62, f32[128,16,128]{2,1,0:T(8,128)S(1)} %get-tuple-element.20, ...), kind=kLoop, calls=%fused_computation.189 | loop fusion | flops 11272192 | bytes 19922944 | tf_op jit(solution)/shard_map/add | solution.py:199
  190.5 0.6 fusion.120
  191.2 0.5 broadcast_select_fusion.3
  191.7 3.6 %collective-permute-start.16 = (f32[128,4,1,128]{3,2,0,1:T(1,128)S(1)}, f32[128,4,1,128]{3,2,0,1:T(1,128)S(1)}, u32[]{:S(2)}, u32[]{:S(2)}) collective-permute-start(f32[128,4,1,128]{3,2,0,1:T(1,128)S(1)} %get-tuple-element.8), channel_id=1, source_target_pairs={{1,2},{5,6},{7,8},{9,10},{13,14},{2,1},{6,5},{8,7},{10,9},{14,13},... | collective-permute-start | bytes 786440 | tf_op jit(solution)/shard_map/ppermute | solution.py:28
  195.4 4.9 %collective-permute-done.16 = f32[128,4,1,128]{3,2,0,1:T(1,128)S(1)} collective-permute-done((f32[128,4,1,128]{3,2,0,1:T(1,128)S(1)}, f32[128,4,1,128]{3,2,0,1:T(1,128)S(1)}, u32[]{:S(2)}, u32[]{:S(2)}) %collective-permute-start.16) | collective-permute-done | bytes 262176 | tf_op jit(solution)/shard_map/ppermute | solution.py:28
  200.4 1.7 maximum_multiply_fusion
  202.1 0.4 slice.605
  202.5 1.7 fusion.82
  204.2 1.9 fusion.8
  206.2 1.9 copy.51
  208.1 3.5 %fusion.196 = f32[16,16,4096]{2,1,0:T(8,128)S(1)} fusion(f32[128,4096,1]{0,1,2:T(8,128)} %bitcast.201, s32[16,16]{1,0:T(8,128)S(1)} %multiply_add_fusion.1, s32[128]{0:T(128)S(1)} %get-tuple-element.102), kind=kOutput, calls=%fused_computation.324 | convolution fusion | flops 1610645504 | bytes 6292992 | tf_op jit(solution)/shard_map/dot_general | solution.py:204
  211.6 96.5 %all_to_all.20 = f32[16,16,4096]{2,1,0:T(8,128)S(1)} all-to-all(f32[16,16,4096]{2,1,0:T(8,128)S(1)} %fusion.196), channel_id=1, replica_groups=mesh['groups'=2,'shot'=16] {'shot'}, dimensions={0} | all-to-all | bytes 8388608 | tf_op jit(solution)/shard_map/all_to_all | solution.py:205
  308.0 1.8 convolution_multiply_fusion
  309.8 1.9 reshape.235
  (93 shorter events, 6.6 us)
Async XLA Ops:
  20.7 7.2 %copy-start.2 = (f32[128,16,128]{2,1,0:T(8,128)S(1)}, f32[128,16,128]{2,1,0:T(8,128)}, u32[]{:S(2)}) copy-start(f32[128,16,128]{2,1,0:T(8,128)} %param.16) | copy-start | bytes 3145732
  20.7 16.2 %copy-start.8 = (f32[1,4]{1,0:T(1,128)S(1)}, f32[1,4]{1,0:T(1,128)}, u32[]{:S(2)}) copy-start(f32[1,4]{1,0:T(1,128)} %param.21) | copy-start | bytes 52
  20.7 16.9 %copy-start.10 = (s32[1,256]{1,0:T(1,128)S(1)}, s32[1,256]{1,0:T(1,128)}, u32[]{:S(2)}) copy-start(s32[1,256]{1,0:T(1,128)} %param.22) | copy-start | bytes 3076
  20.7 16.9 %copy-start.9 = (f32[1,4,256]{2,1,0:T(4,128)S(1)}, f32[1,4,256]{2,1,0:T(4,128)}, u32[]{:S(2)}) copy-start(f32[1,4,256]{2,1,0:T(4,128)} %param.23) | copy-start | bytes 12292
  20.8 101.7 %all-to-all-start.1 = ((f32[16,16,4096]{2,1,0:T(8,128)}), f32[16,16,4096]{2,1,0:T(8,128)}, u32[]{:S(2)}, u32[]{:S(2)}) async-start(f32[16,16,4096]{2,1,0:T(8,128)} %bitcast.195), calls=%async_computation.1 | async-start | bytes 8388608 | tf_op jit(solution)/shard_map/all_to_all | solution.py:143
  28.0 93.0 %collective-permute-start = (f32[128,1,128]{2,1,0:T(1,128)S(1)}, f32[128,1,128]{2,1,0:T(1,128)S(1)}, u32[]{:S(2)}, u32[]{:S(2)}) collective-permute-start(f32[128,1,128]{2,1,0:T(1,128)S(1)} %get-tuple-element.55), channel_id=1, source_target_pairs={{1,2},{5,6},{7,8},{9,10},{13,14},{2,1},{6,5},{8,7},{10,9},{14,13},... | collective-permute-start | bytes 196616 | tf_op jit(solution)/shard_map/ppermute | solution.py:28
  31.4 89.6 %collective-permute-start.1 = (f32[128,1,128]{2,1,0:T(1,128)S(1)}, f32[128,1,128]{2,1,0:T(1,128)S(1)}, u32[]{:S(2)}, u32[]{:S(2)}) collective-permute-start(f32[128,1,128]{2,1,0:T(1,128)S(1)} %get-tuple-element.56), channel_id=1, source_target_pairs={{0,1},{2,3},{4,5},{6,7},{8,9},{10,11},{12,13},{14,15},{1,0},{3,2},... | collective-permute-start | bytes 196616 | tf_op jit(solution)/shard_map/ppermute | solution.py:27
  32.7 89.7 %collective-permute-start.8 = (f32[128,1,128]{2,1,0:T(1,128)S(1)}, f32[128,1,128]{2,1,0:T(1,128)S(1)}, u32[]{:S(2)}, u32[]{:S(2)}) collective-permute-start(f32[128,1,128]{2,1,0:T(1,128)S(1)} %get-tuple-element.35), channel_id=1, source_target_pairs={{1,2},{5,6},{7,8},{9,10},{13,14},{2,1},{6,5},{8,7},{10,9},{14,13},... | collective-permute-start | bytes 196616 | tf_op jit(solution)/shard_map/ppermute | solution.py:28
  36.2 86.2 %collective-permute-start.9 = (f32[128,1,128]{2,1,0:T(1,128)S(1)}, f32[128,1,128]{2,1,0:T(1,128)S(1)}, u32[]{:S(2)}, u32[]{:S(2)}) collective-permute-start(f32[128,1,128]{2,1,0:T(1,128)S(1)} %get-tuple-element.36), channel_id=1, source_target_pairs={{0,1},{2,3},{4,5},{6,7},{8,9},{10,11},{12,13},{14,15},{1,0},{3,2},... | collective-permute-start | bytes 196616 | tf_op jit(solution)/shard_map/ppermute | solution.py:27
  121.3 5.1 %copy-start = (f32[128,18,128]{2,1,0:T(8,128)}, f32[128,18,128]{2,1,0:T(8,128)S(1)}, u32[]{:S(2)}) copy-start(f32[128,18,128]{2,1,0:T(8,128)S(1)} %maximum_multiply_fusion.1) | copy-start | bytes 3538948
  126.6 1.4 copy-start.1
  126.6 1.7 copy-start.4
  126.6 2.0 copy-start.6
  131.1 6.5 %collective-permute-start.2 = (f32[128,1,128]{2,1,0:T(1,128)S(1)}, f32[128,1,128]{2,1,0:T(1,128)S(1)}, u32[]{:S(2)}, u32[]{:S(2)}) collective-permute-start(f32[128,1,128]{2,1,0:T(1,128)S(1)} %get-tuple-element.53), channel_id=1, source_target_pairs={{1,2},{5,6},{7,8},{9,10},{13,14},{2,1},{6,5},{8,7},{10,9},{14,13},... | collective-permute-start | bytes 196616 | tf_op jit(solution)/shard_map/ppermute | solution.py:28
  134.7 2.9 collective-permute-start.3
  134.8 2.9 copy-start.3
  140.7 6.5 %collective-permute-start.4 = (f32[128,1,128]{2,1,0:T(1,128)S(1)}, f32[128,1,128]{2,1,0:T(1,128)S(1)}, u32[]{:S(2)}, u32[]{:S(2)}) collective-permute-start(f32[128,1,128]{2,1,0:T(1,128)S(1)} %get-tuple-element.51), channel_id=1, source_target_pairs={{1,2},{5,6},{7,8},{9,10},{13,14},{2,1},{6,5},{8,7},{10,9},{14,13},... | collective-permute-start | bytes 196616 | tf_op jit(solution)/shard_map/ppermute | solution.py:28
  144.5 2.7 collective-permute-start.5
  150.1 6.5 %collective-permute-start.6 = (f32[128,1,128]{2,1,0:T(1,128)S(1)}, f32[128,1,128]{2,1,0:T(1,128)S(1)}, u32[]{:S(2)}, u32[]{:S(2)}) collective-permute-start(f32[128,1,128]{2,1,0:T(1,128)S(1)} %get-tuple-element.49), channel_id=1, source_target_pairs={{1,2},{5,6},{7,8},{9,10},{13,14},{2,1},{6,5},{8,7},{10,9},{14,13},... | collective-permute-start | bytes 196616 | tf_op jit(solution)/shard_map/ppermute | solution.py:28
  153.7 2.9 collective-permute-start.7
  159.2 1.1 copy-start.5
  162.5 1.2 copy-start.7
  164.6 6.5 %collective-permute-start.10 = (f32[128,1,128]{2,1,0:T(1,128)S(1)}, f32[128,1,128]{2,1,0:T(1,128)S(1)}, u32[]{:S(2)}, u32[]{:S(2)}) collective-permute-start(f32[128,1,128]{2,1,0:T(1,128)S(1)} %get-tuple-element.33), channel_id=1, source_target_pairs={{1,2},{5,6},{7,8},{9,10},{13,14},{2,1},{6,5},{8,7},{10,9},{14,13},... | collective-permute-start | bytes 196616 | tf_op jit(solution)/shard_map/ppermute | solution.py:28
  168.2 2.9 collective-permute-start.11
  172.5 6.5 %collective-permute-start.12 = (f32[128,1,128]{2,1,0:T(1,128)S(1)}, f32[128,1,128]{2,1,0:T(1,128)S(1)}, u32[]{:S(2)}, u32[]{:S(2)}) collective-permute-start(f32[128,1,128]{2,1,0:T(1,128)S(1)} %get-tuple-element.31), channel_id=1, source_target_pairs={{1,2},{5,6},{7,8},{9,10},{13,14},{2,1},{6,5},{8,7},{10,9},{14,13},... | collective-permute-start | bytes 196616 | tf_op jit(solution)/shard_map/ppermute | solution.py:28
  176.3 2.7 collective-permute-start.13
  180.4 6.5 %collective-permute-start.14 = (f32[128,1,128]{2,1,0:T(1,128)S(1)}, f32[128,1,128]{2,1,0:T(1,128)S(1)}, u32[]{:S(2)}, u32[]{:S(2)}) collective-permute-start(f32[128,1,128]{2,1,0:T(1,128)S(1)} %get-tuple-element.29), channel_id=1, source_target_pairs={{1,2},{5,6},{7,8},{9,10},{13,14},{2,1},{6,5},{8,7},{10,9},{14,13},... | collective-permute-start | bytes 196616 | tf_op jit(solution)/shard_map/ppermute | solution.py:28
  184.0 2.9 collective-permute-start.15
  191.7 8.6 %collective-permute-start.16 = (f32[128,4,1,128]{3,2,0,1:T(1,128)S(1)}, f32[128,4,1,128]{3,2,0,1:T(1,128)S(1)}, u32[]{:S(2)}, u32[]{:S(2)}) collective-permute-start(f32[128,4,1,128]{3,2,0,1:T(1,128)S(1)} %get-tuple-element.8), channel_id=1, source_target_pairs={{1,2},{5,6},{7,8},{9,10},{13,14},{2,1},{6,5},{8,7},{10,9},{14,13},... | collective-permute-start | bytes 786440 | tf_op jit(solution)/shard_map/ppermute | solution.py:28
  195.3 5.0 %collective-permute-start.17 = (f32[128,4,1,128]{3,2,0,1:T(1,128)S(1)}, f32[128,4,1,128]{3,2,0,1:T(1,128)S(1)}, u32[]{:S(2)}, u32[]{:S(2)}) collective-permute-start(f32[128,4,1,128]{3,2,0,1:T(1,128)S(1)} %bitcast.228), channel_id=1, source_target_pairs={{0,1},{2,3},{4,5},{6,7},{8,9},{10,11},{12,13},{14,15},{1,0},{3,2},... | collective-permute-start | bytes 786440 | tf_op jit(solution)/shard_map/ppermute | solution.py:27
where the time goes:
time: 314 us; the launch traced here: 312 us
  blocking collectives  107 us (34%)
  waiting for transfers between devices  101 us (32%)
  starting transfers between devices  39.9 us (13%)
  other arithmetic  30.6 us (10%)
  matrix products  20.1 us (6%)
  local copies, waits for them, and re-layouts  11.6 us (4%)
    ppermute x9, waiting for transfers between devices, extended(): got_outer = lax.ppermute(jnp.where(even, leading, last), axis, outer)  101 us
    all_to_all x1, blocking collectives, shards(): lax.all_to_all(returning.reshape(shot_count, capacity, 2 * row_len), 'sho...  96.5 us
    ppermute x9, starting transfers between devices, extended(): got_outer = lax.ppermute(jnp.where(even, leading, last), axis, outer)  32.1 us
    all_to_all x1, blocking collectives, shards(): lax.all_to_all(requests.reshape(shot_count, capacity), 'shot', split_axis...  10.2 us
    add x4, other arithmetic, shards(): advanced = advanced + jnp.where(at_source, wavelet[0, time_step], 0.0)  8.43 us
    all_to_all x1, starting transfers between devices, shards(): lax.all_to_all(outgoing.reshape(shot_count, capacity, 2 * row_len), 'shot...  7.14 us
  transfers between devices with their start and end apart: 19, of which 8 were waited for; matrix products, arithmetic and copies ran while one was open for 2% of the time, Pallas kernels for 0%

commit v1 on v0

--- a/solution.py
+++ b/solution.py
@@ -201,7 +201,7 @@
     stacked = jnp.stack([gradient_speed, gradient_aniso, speeds, jnp.ones_like(speeds)], axis=1)
     smoothed = diffuse(image_rims_of(stacked))
     rows_out = smoothed.reshape(NEED, 2 * row_len)
-    returning = jnp.dot(place_hot.T, rows_out, precision=lax.Precision.HIGHEST)
+    returning = select_dot(place_hot.T, rows_out)
     returned = lax.all_to_all(
         returning.reshape(shot_count, capacity, 2 * row_len),
         "shot",

time: 314 us -> 315 us (level)
  other arithmetic: 30.6 us -> 34.1 us
    dot_general x1 -> x0, matrix products: 3.49 us -> none  [shards(): returning = jnp.dot(place_hot.T, rows_out, precision=lax.Precision.HIGHEST)]
    dot_general x8 -> x9, matrix products: 5.85 us -> 7.63 us  [select_dot(): jnp.dot(hot.astype(jnp.bfloat16), split3(values), preferred_element_type=...]
where the time goes in v1:
time: 315 us; the launch traced here: 313 us
  blocking collectives  107 us (34%)
  waiting for transfers between devices  101 us (32%)
  starting transfers between devices  39.9 us (13%)
  other arithmetic  34.1 us (11%)
  matrix products  18.4 us (6%)
  local copies, waits for them, and re-layouts  11.1 us (4%)
    ppermute x9, waiting for transfers between devices, extended(): got_outer = lax.ppermute(jnp.where(even, leading, last), axis, outer)  101 us
    all_to_all x1, blocking collectives, shards(): lax.all_to_all(returning.reshape(shot_count, capacity, 2 * row_len), 'sho...  96.5 us
    ppermute x9, starting transfers between devices, extended(): got_outer = lax.ppermute(jnp.where(even, leading, last), axis, outer)  32.1 us
    all_to_all x1, blocking collectives, shards(): lax.all_to_all(requests.reshape(shot_count, capacity), 'shot', split_axis...  10.2 us
    add x4, other arithmetic, shards(): advanced = advanced + jnp.where(at_source, wavelet[0, time_step], 0.0)  8.35 us
    dot_general x9, matrix products, select_dot(): jnp.dot(hot.astype(jnp.bfloat16), split3(values), preferred_element_type=...  7.63 us
    all_to_all x1, starting transfers between devices, shards(): lax.all_to_all(outgoing.reshape(shot_count, capacity, 2 * row_len), 'shot...  7.15 us
  transfers between devices with their start and end apart: 19, of which 8 were waited for; matrix products, arithmetic and copies ran while one was open for 2% of the time, Pallas kernels for 0%

profile of v1, /device:TPU:13, one launch (start us, length us, event | category | flops | bytes accessed | tf_op | source)
XLA Modules:
  0.0 313.0 jit_solution(7885701620150537814)
XLA Ops:
  0.6 0.7 fusion.207
  1.5 0.8 select_reduce_fusion
  2.4 0.7 fusion.221
  3.0 1.1 scatter_custom_fusion
  4.2 10.2 %all_to_all.19 = s32[16,1,16]{2,1,0:T(1,128)S(1)} all-to-all(s32[16,1,16]{2,1,0:T(1,128)S(1)} %all_to_all.12), channel_id=1, replica_groups=mesh['groups'=2,'shot'=16] {'shot'}, dimensions={0} | all-to-all | bytes 2048 | tf_op jit(solution)/shard_map/all_to_all | solution.py:134
  14.4 0.5 broadcast.267
  14.9 0.7 reduce.3
  15.7 5.1 %fusion.156 = f32[256,4096]{1,0:T(8,128)} fusion(f32[64,2048]{1,0:T(8,128)} %param.13, f32[64,2048]{1,0:T(8,128)} %param.12, s32[256]{0:T(256)S(1)} %eq.131), kind=kOutput, calls=%fused_computation.253 | convolution fusion | flops 805584896 | bytes 5243904 | tf_op jit(solution)/shard_map/dot_general | solution.py:142
  20.8 7.1 %all-to-all-start.1 = ((f32[16,16,4096]{2,1,0:T(8,128)}), f32[16,16,4096]{2,1,0:T(8,128)}, u32[]{:S(2)}, u32[]{:S(2)}) async-start(f32[16,16,4096]{2,1,0:T(8,128)} %bitcast.199), calls=%async_computation.1 | async-start | bytes 8388608 | tf_op jit(solution)/shard_map/all_to_all | solution.py:143
  28.0 3.4 %collective-permute-start = (f32[128,1,128]{2,1,0:T(1,128)S(1)}, f32[128,1,128]{2,1,0:T(1,128)S(1)}, u32[]{:S(2)}, u32[]{:S(2)}) collective-permute-start(f32[128,1,128]{2,1,0:T(1,128)S(1)} %get-tuple-element.58), channel_id=1, source_target_pairs={{1,2},{5,6},{7,8},{9,10},{13,14},{2,1},{6,5},{8,7},{10,9},{14,13},... | collective-permute-start | bytes 196616 | tf_op jit(solution)/shard_map/ppermute | solution.py:28
  31.4 1.3 broadcast_select_fusion.19
  32.7 3.5 %collective-permute-start.8 = (f32[128,1,128]{2,1,0:T(1,128)S(1)}, f32[128,1,128]{2,1,0:T(1,128)S(1)}, u32[]{:S(2)}, u32[]{:S(2)}) collective-permute-start(f32[128,1,128]{2,1,0:T(1,128)S(1)} %get-tuple-element.38), channel_id=1, source_target_pairs={{1,2},{5,6},{7,8},{9,10},{13,14},{2,1},{6,5},{8,7},{10,9},{14,13},... | collective-permute-start | bytes 196616 | tf_op jit(solution)/shard_map/ppermute | solution.py:28
  37.0 0.6 fusion.228
  37.7 83.3 %collective-permute-done = f32[128,1,128]{2,1,0:T(1,128)S(1)} collective-permute-done((f32[128,1,128]{2,1,0:T(1,128)S(1)}, f32[128,1,128]{2,1,0:T(1,128)S(1)}, u32[]{:S(2)}, u32[]{:S(2)}) %collective-permute-start) | collective-permute-done | bytes 65568 | tf_op jit(solution)/shard_map/ppermute | solution.py:28
  121.3 1.1 slice.556
  122.4 3.9 %fusion.202 = f32[128,4096]{1,0:T(8,128)S(1)} fusion(f32[256,4096]{1,0:T(8,128)} %bitcast.5, s32[128]{0:T(128)S(1)} %get-tuple-element.105), kind=kOutput, calls=%fused_computation.338 | convolution fusion | flops 1610645504 | bytes 6291968 | tf_op jit(solution)/shard_map/dot_general | solution.py:153
  126.9 0.8 copy-done.2
  127.7 0.3 copy-done.4
  128.1 2.0 fusion.113
  130.5 3.6 %collective-permute-start.2 = (f32[128,1,128]{2,1,0:T(1,128)S(1)}, f32[128,1,128]{2,1,0:T(1,128)S(1)}, u32[]{:S(2)}, u32[]{:S(2)}) collective-permute-start(f32[128,1,128]{2,1,0:T(1,128)S(1)} %get-tuple-element.56), channel_id=1, source_target_pairs={{1,2},{5,6},{7,8},{9,10},{13,14},{2,1},{6,5},{8,7},{10,9},{14,13},... | collective-permute-start | bytes 196616 | tf_op jit(solution)/shard_map/ppermute | solution.py:28
  134.1 0.8 fusion.28
  134.9 2.1 collective-permute-done.2
  137.0 0.6 maximum_multiply_fusion.5
  137.6 2.1 fusion.117
  140.1 3.7 %collective-permute-start.4 = (f32[128,1,128]{2,1,0:T(1,128)S(1)}, f32[128,1,128]{2,1,0:T(1,128)S(1)}, u32[]{:S(2)}, u32[]{:S(2)}) collective-permute-start(f32[128,1,128]{2,1,0:T(1,128)S(1)} %get-tuple-element.54), channel_id=1, source_target_pairs={{1,2},{5,6},{7,8},{9,10},{13,14},{2,1},{6,5},{8,7},{10,9},{14,13},... | collective-permute-start | bytes 196616 | tf_op jit(solution)/shard_map/ppermute | solution.py:28
  143.9 0.8 fusion.29
  144.8 1.8 collective-permute-done.4
  147.0 2.1 fusion.121
  149.6 3.6 %collective-permute-start.6 = (f32[128,1,128]{2,1,0:T(1,128)S(1)}, f32[128,1,128]{2,1,0:T(1,128)S(1)}, u32[]{:S(2)}, u32[]{:S(2)}) collective-permute-start(f32[128,1,128]{2,1,0:T(1,128)S(1)} %get-tuple-element.52), channel_id=1, source_target_pairs={{1,2},{5,6},{7,8},{9,10},{13,14},{2,1},{6,5},{8,7},{10,9},{14,13},... | collective-permute-start | bytes 196616 | tf_op jit(solution)/shard_map/ppermute | solution.py:28
  153.2 0.8 fusion.30
  154.0 2.1 collective-permute-done.6
  156.5 2.1 fusion.125
  158.9 0.8 fusion.31
  159.7 0.3 fusion.201
  160.3 0.7 fusion.25
  161.2 0.7 fusion.27
  162.0 1.1 copy-done.5
  163.1 0.9 fusion.69
  164.1 3.6 %collective-permute-start.10 = (f32[128,1,128]{2,1,0:T(1,128)S(1)}, f32[128,1,128]{2,1,0:T(1,128)S(1)}, u32[]{:S(2)}, u32[]{:S(2)}) collective-permute-start(f32[128,1,128]{2,1,0:T(1,128)S(1)} %get-tuple-element.36), channel_id=1, source_target_pairs={{1,2},{5,6},{7,8},{9,10},{13,14},{2,1},{6,5},{8,7},{10,9},{14,13},... | collective-permute-start | bytes 196616 | tf_op jit(solution)/shard_map/ppermute | solution.py:28
  167.8 0.7 fusion.26
  168.6 2.0 collective-permute-done.10
  171.0 1.0 fusion.75
  172.2 3.8 %collective-permute-start.12 = (f32[128,1,128]{2,1,0:T(1,128)S(1)}, f32[128,1,128]{2,1,0:T(1,128)S(1)}, u32[]{:S(2)}, u32[]{:S(2)}) collective-permute-start(f32[128,1,128]{2,1,0:T(1,128)S(1)} %get-tuple-element.34), channel_id=1, source_target_pairs={{1,2},{5,6},{7,8},{9,10},{13,14},{2,1},{6,5},{8,7},{10,9},{14,13},... | collective-permute-start | bytes 196616 | tf_op jit(solution)/shard_map/ppermute | solution.py:28
  176.0 0.7 fusion.24
  176.7 1.9 collective-permute-done.12
  179.1 0.9 fusion.81
  180.1 3.6 %collective-permute-start.14 = (f32[128,1,128]{2,1,0:T(1,128)S(1)}, f32[128,1,128]{2,1,0:T(1,128)S(1)}, u32[]{:S(2)}, u32[]{:S(2)}) collective-permute-start(f32[128,1,128]{2,1,0:T(1,128)S(1)} %get-tuple-element.32), channel_id=1, source_target_pairs={{1,2},{5,6},{7,8},{9,10},{13,14},{2,1},{6,5},{8,7},{10,9},{14,13},... | collective-permute-start | bytes 196616 | tf_op jit(solution)/shard_map/ppermute | solution.py:28
  183.8 2.7 collective-permute-done.14
  187.0 3.2 %fusion.126 = (f32[128,16,128]{2,1,0:T(8,128)S(1)}, f32[128,16,128]{2,1,0:T(8,128)S(1)}) fusion(f32[16,8,16,128]{3,2,1,0:T(8,128)S(1)} %copy.52, f32[128,16,128]{2,1,0:T(8,128)S(1)} %fusion.81, f32[128,16,128]{2,1,0:T(8,128)S(1)} %fusion.75, f32[128,16,128]{2,1,0:T(8,128)S(1)} %fusion.69, f32[128,16,128]{2,1,0:T(8,128)S(1)} %get-tuple-element.20, ...), kind=kLoop, calls=%fused_computation.202 | loop fusion | flops 11272192 | bytes 19922944 | tf_op jit(solution)/shard_map/add | solution.py:199
  190.2 0.6 fusion.127
  190.9 0.5 broadcast_select_fusion.3
  191.3 3.6 %collective-permute-start.16 = (f32[128,4,1,128]{3,2,0,1:T(1,128)S(1)}, f32[128,4,1,128]{3,2,0,1:T(1,128)S(1)}, u32[]{:S(2)}, u32[]{:S(2)}) collective-permute-start(f32[128,4,1,128]{3,2,0,1:T(1,128)S(1)} %get-tuple-element.8), channel_id=1, source_target_pairs={{1,2},{5,6},{7,8},{9,10},{13,14},{2,1},{6,5},{8,7},{10,9},{14,13},... | collective-permute-start | bytes 786440 | tf_op jit(solution)/shard_map/ppermute | solution.py:28
  195.0 4.9 %collective-permute-done.16 = f32[128,4,1,128]{3,2,0,1:T(1,128)S(1)} collective-permute-done((f32[128,4,1,128]{3,2,0,1:T(1,128)S(1)}, f32[128,4,1,128]{3,2,0,1:T(1,128)S(1)}, u32[]{:S(2)}, u32[]{:S(2)}) %collective-permute-start.16) | collective-permute-done | bytes 262176 | tf_op jit(solution)/shard_map/ppermute | solution.py:28
  200.0 1.7 maximum_multiply_fusion
  201.7 0.4 slice.617
  202.1 1.7 fusion.89
  203.8 2.0 fusion.15
  205.7 1.9 copy.50
  207.6 2.1 reduce-precision_convert_fusion.1
  209.8 1.8 fusion
  211.6 1.2 slice_add_fusion
  212.8 96.5 %all_to_all.20 = f32[16,16,4096]{2,1,0:T(8,128)S(1)} all-to-all(f32[16,16,4096]{2,1,0:T(8,128)S(1)} %bitcast.201), channel_id=1, replica_groups=mesh['groups'=2,'shot'=16] {'shot'}, dimensions={0} | all-to-all | bytes 8388608 | tf_op jit(solution)/shard_map/all_to_all | solution.py:205
  309.3 1.8 convolution_multiply_fusion
  311.1 1.9 reshape.220
  (90 shorter events, 6.9 us)
Async XLA Ops:
  20.7 7.2 %copy-start = (f32[128,16,128]{2,1,0:T(8,128)S(1)}, f32[128,16,128]{2,1,0:T(8,128)}, u32[]{:S(2)}) copy-start(f32[128,16,128]{2,1,0:T(8,128)} %param.16) | copy-start | bytes 3145732
  20.7 16.3 %copy-start.6 = (f32[1,4]{1,0:T(1,128)S(1)}, f32[1,4]{1,0:T(1,128)}, u32[]{:S(2)}) copy-start(f32[1,4]{1,0:T(1,128)} %param.21) | copy-start | bytes 52
  20.7 16.9 %copy-start.8 = (s32[1,256]{1,0:T(1,128)S(1)}, s32[1,256]{1,0:T(1,128)}, u32[]{:S(2)}) copy-start(s32[1,256]{1,0:T(1,128)} %param.22) | copy-start | bytes 3076
  20.8 16.9 %copy-start.7 = (f32[1,4,256]{2,1,0:T(4,128)S(1)}, f32[1,4,256]{2,1,0:T(4,128)}, u32[]{:S(2)}) copy-start(f32[1,4,256]{2,1,0:T(4,128)} %param.23) | copy-start | bytes 12292
  20.8 101.6 %all-to-all-start.1 = ((f32[16,16,4096]{2,1,0:T(8,128)}), f32[16,16,4096]{2,1,0:T(8,128)}, u32[]{:S(2)}, u32[]{:S(2)}) async-start(f32[16,16,4096]{2,1,0:T(8,128)} %bitcast.199), calls=%async_computation.1 | async-start | bytes 8388608 | tf_op jit(solution)/shard_map/all_to_all | solution.py:143
  28.0 93.0 %collective-permute-start = (f32[128,1,128]{2,1,0:T(1,128)S(1)}, f32[128,1,128]{2,1,0:T(1,128)S(1)}, u32[]{:S(2)}, u32[]{:S(2)}) collective-permute-start(f32[128,1,128]{2,1,0:T(1,128)S(1)} %get-tuple-element.58), channel_id=1, source_target_pairs={{1,2},{5,6},{7,8},{9,10},{13,14},{2,1},{6,5},{8,7},{10,9},{14,13},... | collective-permute-start | bytes 196616 | tf_op jit(solution)/shard_map/ppermute | solution.py:28
  31.4 89.6 %collective-permute-start.1 = (f32[128,1,128]{2,1,0:T(1,128)S(1)}, f32[128,1,128]{2,1,0:T(1,128)S(1)}, u32[]{:S(2)}, u32[]{:S(2)}) collective-permute-start(f32[128,1,128]{2,1,0:T(1,128)S(1)} %get-tuple-element.59), channel_id=1, source_target_pairs={{0,1},{2,3},{4,5},{6,7},{8,9},{10,11},{12,13},{14,15},{1,0},{3,2},... | collective-permute-start | bytes 196616 | tf_op jit(solution)/shard_map/ppermute | solution.py:27
  32.7 89.6 %collective-permute-start.8 = (f32[128,1,128]{2,1,0:T(1,128)S(1)}, f32[128,1,128]{2,1,0:T(1,128)S(1)}, u32[]{:S(2)}, u32[]{:S(2)}) collective-permute-start(f32[128,1,128]{2,1,0:T(1,128)S(1)} %get-tuple-element.38), channel_id=1, source_target_pairs={{1,2},{5,6},{7,8},{9,10},{13,14},{2,1},{6,5},{8,7},{10,9},{14,13},... | collective-permute-start | bytes 196616 | tf_op jit(solution)/shard_map/ppermute | solution.py:28
  36.2 86.1 %collective-permute-start.9 = (f32[128,1,128]{2,1,0:T(1,128)S(1)}, f32[128,1,128]{2,1,0:T(1,128)S(1)}, u32[]{:S(2)}, u32[]{:S(2)}) collective-permute-start(f32[128,1,128]{2,1,0:T(1,128)S(1)} %get-tuple-element.39), channel_id=1, source_target_pairs={{0,1},{2,3},{4,5},{6,7},{8,9},{10,11},{12,13},{14,15},{1,0},{3,2},... | collective-permute-start | bytes 196616 | tf_op jit(solution)/shard_map/ppermute | solution.py:27
  126.5 1.2 copy-start.2
  126.5 1.5 copy-start.4
  130.5 6.5 %collective-permute-start.2 = (f32[128,1,128]{2,1,0:T(1,128)S(1)}, f32[128,1,128]{2,1,0:T(1,128)S(1)}, u32[]{:S(2)}, u32[]{:S(2)}) collective-permute-start(f32[128,1,128]{2,1,0:T(1,128)S(1)} %get-tuple-element.56), channel_id=1, source_target_pairs={{1,2},{5,6},{7,8},{9,10},{13,14},{2,1},{6,5},{8,7},{10,9},{14,13},... | collective-permute-start | bytes 196616 | tf_op jit(solution)/shard_map/ppermute | solution.py:28
  134.0 2.9 collective-permute-start.3
  134.1 2.9 copy-start.1
  140.1 6.5 %collective-permute-start.4 = (f32[128,1,128]{2,1,0:T(1,128)S(1)}, f32[128,1,128]{2,1,0:T(1,128)S(1)}, u32[]{:S(2)}, u32[]{:S(2)}) collective-permute-start(f32[128,1,128]{2,1,0:T(1,128)S(1)} %get-tuple-element.54), channel_id=1, source_target_pairs={{1,2},{5,6},{7,8},{9,10},{13,14},{2,1},{6,5},{8,7},{10,9},{14,13},... | collective-permute-start | bytes 196616 | tf_op jit(solution)/shard_map/ppermute | solution.py:28
  143.9 2.7 collective-permute-start.5
  149.6 6.5 %collective-permute-start.6 = (f32[128,1,128]{2,1,0:T(1,128)S(1)}, f32[128,1,128]{2,1,0:T(1,128)S(1)}, u32[]{:S(2)}, u32[]{:S(2)}) collective-permute-start(f32[128,1,128]{2,1,0:T(1,128)S(1)} %get-tuple-element.52), channel_id=1, source_target_pairs={{1,2},{5,6},{7,8},{9,10},{13,14},{2,1},{6,5},{8,7},{10,9},{14,13},... | collective-permute-start | bytes 196616 | tf_op jit(solution)/shard_map/ppermute | solution.py:28
  153.1 2.9 collective-permute-start.7
  158.6 1.1 copy-start.3
  161.9 1.2 copy-start.5
  164.1 6.5 %collective-permute-start.10 = (f32[128,1,128]{2,1,0:T(1,128)S(1)}, f32[128,1,128]{2,1,0:T(1,128)S(1)}, u32[]{:S(2)}, u32[]{:S(2)}) collective-permute-start(f32[128,1,128]{2,1,0:T(1,128)S(1)} %get-tuple-element.36), channel_id=1, source_target_pairs={{1,2},{5,6},{7,8},{9,10},{13,14},{2,1},{6,5},{8,7},{10,9},{14,13},... | collective-permute-start | bytes 196616 | tf_op jit(solution)/shard_map/ppermute | solution.py:28
  167.7 2.9 collective-permute-start.11
  172.2 6.5 %collective-permute-start.12 = (f32[128,1,128]{2,1,0:T(1,128)S(1)}, f32[128,1,128]{2,1,0:T(1,128)S(1)}, u32[]{:S(2)}, u32[]{:S(2)}) collective-permute-start(f32[128,1,128]{2,1,0:T(1,128)S(1)} %get-tuple-element.34), channel_id=1, source_target_pairs={{1,2},{5,6},{7,8},{9,10},{13,14},{2,1},{6,5},{8,7},{10,9},{14,13},... | collective-permute-start | bytes 196616 | tf_op jit(solution)/shard_map/ppermute | solution.py:28
  175.9 2.7 collective-permute-start.13
  180.1 6.5 %collective-permute-start.14 = (f32[128,1,128]{2,1,0:T(1,128)S(1)}, f32[128,1,128]{2,1,0:T(1,128)S(1)}, u32[]{:S(2)}, u32[]{:S(2)}) collective-permute-start(f32[128,1,128]{2,1,0:T(1,128)S(1)} %get-tuple-element.32), channel_id=1, source_target_pairs={{1,2},{5,6},{7,8},{9,10},{13,14},{2,1},{6,5},{8,7},{10,9},{14,13},... | collective-permute-start | bytes 196616 | tf_op jit(solution)/shard_map/ppermute | solution.py:28
  183.6 2.9 collective-permute-start.15
  191.3 8.6 %collective-permute-start.16 = (f32[128,4,1,128]{3,2,0,1:T(1,128)S(1)}, f32[128,4,1,128]{3,2,0,1:T(1,128)S(1)}, u32[]{:S(2)}, u32[]{:S(2)}) collective-permute-start(f32[128,4,1,128]{3,2,0,1:T(1,128)S(1)} %get-tuple-element.8), channel_id=1, source_target_pairs={{1,2},{5,6},{7,8},{9,10},{13,14},{2,1},{6,5},{8,7},{10,9},{14,13},... | collective-permute-start | bytes 786440 | tf_op jit(solution)/shard_map/ppermute | solution.py:28
  194.9 5.0 %collective-permute-start.17 = (f32[128,4,1,128]{3,2,0,1:T(1,128)S(1)}, f32[128,4,1,128]{3,2,0,1:T(1,128)S(1)}, u32[]{:S(2)}, u32[]{:S(2)}) collective-permute-start(f32[128,4,1,128]{3,2,0,1:T(1,128)S(1)} %bitcast.232), channel_id=1, source_target_pairs={{0,1},{2,3},{4,5},{6,7},{8,9},{10,11},{12,13},{14,15},{1,0},{3,2},... | collective-permute-start | bytes 786440 | tf_op jit(solution)/shard_map/ppermute | solution.py:27

commit v2 on v0

--- a/solution.py
+++ b/solution.py
@@ -198,8 +198,16 @@
         later_adjoint, adjoint = (adjoint, earlier)
     gradient_speed = hfactor * image_horizontal + image_vertical
     gradient_aniso = 2.0 * speeds * image_horizontal
-    stacked = jnp.stack([gradient_speed, gradient_aniso, speeds, jnp.ones_like(speeds)], axis=1)
-    smoothed = diffuse(image_rims_of(stacked))
+    stacked = jnp.stack([gradient_speed, gradient_aniso, speeds], axis=1)
+    widened = image_rims_of(stacked)
+    me = lax.axis_index("shot")
+    position = (me + SPLIT // 2) % SPLIT
+    layer = lax.broadcasted_iota(jnp.int32, (1, 1, widened.shape[2], 1), 2)
+    has_below = jnp.logical_and(position > 0, me > 0)
+    has_above = jnp.logical_and(position < SPLIT - 1, me < shot_count - 1)
+    exists = jnp.where(layer == 0, has_below, jnp.where(layer == widened.shape[2] - 1, has_above, True))
+    ones = jnp.broadcast_to(exists.astype(jnp.float32), widened[:, :1].shape)
+    smoothed = diffuse(jnp.concatenate([widened, ones], axis=1))
     rows_out = smoothed.reshape(NEED, 2 * row_len)
     returning = jnp.dot(place_hot.T, rows_out, precision=lax.Precision.HIGHEST)
     returned = lax.all_to_all(

time: 314 us -> 313 us (level)
  transfers between devices with their start and end apart: 19 -> 19, of which waited for: 8 -> 8; matrix products, arithmetic and copies ran while one was open for 2% -> 3% of each run, Pallas kernels for 0% -> 0%
where the time goes in v2:
time: 313 us; the launch traced here: 311 us
  blocking collectives  108 us (35%)
  waiting for transfers between devices  99.3 us (32%)
  starting transfers between devices  39.9 us (13%)
  other arithmetic  30.6 us (10%)
  matrix products  20.1 us (6%)
  local copies, waits for them, and re-layouts  10.8 us (3%)
    ppermute x9, waiting for transfers between devices, extended(): got_outer = lax.ppermute(jnp.where(even, leading, last), axis, outer)  99.3 us
    all_to_all x1, blocking collectives, shards(): lax.all_to_all(returning.reshape(shot_count, capacity, 2 * row_len), 'sho...  97.7 us
    ppermute x9, starting transfers between devices, extended(): got_outer = lax.ppermute(jnp.where(even, leading, last), axis, outer)  32.1 us
    all_to_all x1, blocking collectives, shards(): lax.all_to_all(requests.reshape(shot_count, capacity), 'shot', split_axis...  10.2 us
    add x4, other arithmetic, shards(): advanced = advanced + jnp.where(at_source, wavelet[0, time_step], 0.0)  8.35 us
    all_to_all x1, starting transfers between devices, shards(): lax.all_to_all(outgoing.reshape(shot_count, capacity, 2 * row_len), 'shot...  7.15 us
  transfers between devices with their start and end apart: 19, of which 8 were waited for; matrix products, arithmetic and copies ran while one was open for 3% of the time, Pallas kernels for 0%

profile of v2, /device:TPU:13, one launch (start us, length us, event | category | flops | bytes accessed | tf_op | source)
XLA Modules:
  0.0 310.7 jit_solution(11878804164550723825)
XLA Ops:
  0.6 0.7 fusion.203
  1.5 0.8 select_reduce_fusion
  2.4 0.7 fusion.216
  3.0 1.1 scatter_custom_fusion
  4.2 10.2 %all_to_all.19 = s32[16,1,16]{2,1,0:T(1,128)S(1)} all-to-all(s32[16,1,16]{2,1,0:T(1,128)S(1)} %all_to_all.12), channel_id=1, replica_groups=mesh['groups'=2,'shot'=16] {'shot'}, dimensions={0} | all-to-all | bytes 2048 | tf_op jit(solution)/shard_map/all_to_all | solution.py:134
  14.4 0.5 broadcast.345
  14.9 0.7 reduce.3
  15.7 5.1 %fusion.149 = f32[256,4096]{1,0:T(8,128)} fusion(f32[64,2048]{1,0:T(8,128)} %param.13, f32[64,2048]{1,0:T(8,128)} %param.12, s32[256]{0:T(256)S(1)} %eq.175), kind=kOutput, calls=%fused_computation.241 | convolution fusion | flops 805584896 | bytes 5243904 | tf_op jit(solution)/shard_map/dot_general | solution.py:142
  20.8 7.1 %all-to-all-start.1 = ((f32[16,16,4096]{2,1,0:T(8,128)}), f32[16,16,4096]{2,1,0:T(8,128)}, u32[]{:S(2)}, u32[]{:S(2)}) async-start(f32[16,16,4096]{2,1,0:T(8,128)} %bitcast.199), calls=%async_computation.1 | async-start | bytes 8388608 | tf_op jit(solution)/shard_map/all_to_all | solution.py:143
  28.0 3.4 %collective-permute-start = (f32[128,1,128]{2,1,0:T(1,128)S(1)}, f32[128,1,128]{2,1,0:T(1,128)S(1)}, u32[]{:S(2)}, u32[]{:S(2)}) collective-permute-start(f32[128,1,128]{2,1,0:T(1,128)S(1)} %get-tuple-element.55), channel_id=1, source_target_pairs={{1,2},{5,6},{7,8},{9,10},{13,14},{2,1},{6,5},{8,7},{10,9},{14,13},... | collective-permute-start | bytes 196616 | tf_op jit(solution)/shard_map/ppermute | solution.py:28
  31.5 1.3 broadcast_select_fusion.19
  32.8 3.5 %collective-permute-start.8 = (f32[128,1,128]{2,1,0:T(1,128)S(1)}, f32[128,1,128]{2,1,0:T(1,128)S(1)}, u32[]{:S(2)}, u32[]{:S(2)}) collective-permute-start(f32[128,1,128]{2,1,0:T(1,128)S(1)} %get-tuple-element.35), channel_id=1, source_target_pairs={{1,2},{5,6},{7,8},{9,10},{13,14},{2,1},{6,5},{8,7},{10,9},{14,13},... | collective-permute-start | bytes 196616 | tf_op jit(solution)/shard_map/ppermute | solution.py:28
  37.1 0.6 fusion.223
  37.7 83.2 %collective-permute-done = f32[128,1,128]{2,1,0:T(1,128)S(1)} collective-permute-done((f32[128,1,128]{2,1,0:T(1,128)S(1)}, f32[128,1,128]{2,1,0:T(1,128)S(1)}, u32[]{:S(2)}, u32[]{:S(2)}) %collective-permute-start) | collective-permute-done | bytes 65568 | tf_op jit(solution)/shard_map/ppermute | solution.py:28
  121.0 0.3 maximum_multiply_fusion.1
  121.3 1.1 slice.562
  122.4 3.9 %fusion.195 = f32[128,4096]{1,0:T(8,128)S(1)} fusion(f32[256,4096]{1,0:T(8,128)} %bitcast.5, s32[128]{0:T(128)S(1)} %get-tuple-element.102), kind=kOutput, calls=%fused_computation.323 | convolution fusion | flops 1610645504 | bytes 6291968 | tf_op jit(solution)/shard_map/dot_general | solution.py:153
  126.9 0.8 copy-done.2
  127.8 0.3 copy-done.4
  128.1 2.0 fusion.106
  130.5 3.6 %collective-permute-start.2 = (f32[128,1,128]{2,1,0:T(1,128)S(1)}, f32[128,1,128]{2,1,0:T(1,128)S(1)}, u32[]{:S(2)}, u32[]{:S(2)}) collective-permute-start(f32[128,1,128]{2,1,0:T(1,128)S(1)} %get-tuple-element.53), channel_id=1, source_target_pairs={{1,2},{5,6},{7,8},{9,10},{13,14},{2,1},{6,5},{8,7},{10,9},{14,13},... | collective-permute-start | bytes 196616 | tf_op jit(solution)/shard_map/ppermute | solution.py:28
  134.1 0.8 fusion.21
  134.9 2.1 collective-permute-done.2
  137.0 0.6 maximum_multiply_fusion.5
  137.6 2.1 fusion.110
  140.1 3.7 %collective-permute-start.4 = (f32[128,1,128]{2,1,0:T(1,128)S(1)}, f32[128,1,128]{2,1,0:T(1,128)S(1)}, u32[]{:S(2)}, u32[]{:S(2)}) collective-permute-start(f32[128,1,128]{2,1,0:T(1,128)S(1)} %get-tuple-element.51), channel_id=1, source_target_pairs={{1,2},{5,6},{7,8},{9,10},{13,14},{2,1},{6,5},{8,7},{10,9},{14,13},... | collective-permute-start | bytes 196616 | tf_op jit(solution)/shard_map/ppermute | solution.py:28
  144.0 0.8 fusion.22
  144.8 1.8 collective-permute-done.4
  146.6 0.3 maximum_multiply_fusion.3
  147.0 2.1 fusion.114
  149.6 3.6 %collective-permute-start.6 = (f32[128,1,128]{2,1,0:T(1,128)S(1)}, f32[128,1,128]{2,1,0:T(1,128)S(1)}, u32[]{:S(2)}, u32[]{:S(2)}) collective-permute-start(f32[128,1,128]{2,1,0:T(1,128)S(1)} %get-tuple-element.49), channel_id=1, source_target_pairs={{1,2},{5,6},{7,8},{9,10},{13,14},{2,1},{6,5},{8,7},{10,9},{14,13},... | collective-permute-start | bytes 196616 | tf_op jit(solution)/shard_map/ppermute | solution.py:28
  153.2 0.8 fusion.23
  154.0 2.1 collective-permute-done.6
  156.5 2.1 fusion.118
  158.9 0.8 fusion.24
  159.7 0.3 fusion.194
  160.3 0.7 fusion.20
  161.2 1.1 copy-done.5
  162.3 1.0 fusion.62
  163.4 3.6 %collective-permute-start.10 = (f32[128,1,128]{2,1,0:T(1,128)S(1)}, f32[128,1,128]{2,1,0:T(1,128)S(1)}, u32[]{:S(2)}, u32[]{:S(2)}) collective-permute-start(f32[128,1,128]{2,1,0:T(1,128)S(1)} %get-tuple-element.33), channel_id=1, source_target_pairs={{1,2},{5,6},{7,8},{9,10},{13,14},{2,1},{6,5},{8,7},{10,9},{14,13},... | collective-permute-start | bytes 196616 | tf_op jit(solution)/shard_map/ppermute | solution.py:28
  167.0 0.7 fusion.19
  167.9 0.7 fusion.18
  168.7 1.1 collective-permute-done.10
  170.3 1.0 fusion.68
  171.4 3.8 %collective-permute-start.12 = (f32[128,1,128]{2,1,0:T(1,128)S(1)}, f32[128,1,128]{2,1,0:T(1,128)S(1)}, u32[]{:S(2)}, u32[]{:S(2)}) collective-permute-start(f32[128,1,128]{2,1,0:T(1,128)S(1)} %get-tuple-element.31), channel_id=1, source_target_pairs={{1,2},{5,6},{7,8},{9,10},{13,14},{2,1},{6,5},{8,7},{10,9},{14,13},... | collective-permute-start | bytes 196616 | tf_op jit(solution)/shard_map/ppermute | solution.py:28
  175.2 0.7 fusion.17
  176.0 1.9 collective-permute-done.12
  178.3 0.9 fusion.74
  179.3 3.6 %collective-permute-start.14 = (f32[128,1,128]{2,1,0:T(1,128)S(1)}, f32[128,1,128]{2,1,0:T(1,128)S(1)}, u32[]{:S(2)}, u32[]{:S(2)}) collective-permute-start(f32[128,1,128]{2,1,0:T(1,128)S(1)} %get-tuple-element.29), channel_id=1, source_target_pairs={{1,2},{5,6},{7,8},{9,10},{13,14},{2,1},{6,5},{8,7},{10,9},{14,13},... | collective-permute-start | bytes 196616 | tf_op jit(solution)/shard_map/ppermute | solution.py:28
  183.1 2.7 collective-permute-done.14
  186.2 3.2 %fusion.119 = (f32[128,16,128]{2,1,0:T(8,128)S(1)}, f32[128,16,128]{2,1,0:T(8,128)S(1)}) fusion(f32[16,8,16,128]{3,2,1,0:T(8,128)S(1)} %copy.56, f32[128,16,128]{2,1,0:T(8,128)S(1)} %fusion.74, f32[128,16,128]{2,1,0:T(8,128)S(1)} %fusion.68, f32[128,16,128]{2,1,0:T(8,128)S(1)} %fusion.62, f32[128,16,128]{2,1,0:T(8,128)S(1)} %get-tuple-element.20, ...), kind=kLoop, calls=%fused_computation.190 | loop fusion | flops 11272192 | bytes 19922944 | tf_op jit(solution)/shard_map/add | solution.py:199
  189.4 0.6 fusion.120
  190.0 0.3 broadcast_select_fusion.3
  190.5 3.6 %collective-permute-start.16 = (f32[128,3,1,128]{3,2,0,1:T(1,128)S(1)}, f32[128,3,1,128]{3,2,0,1:T(1,128)S(1)}, u32[]{:S(2)}, u32[]{:S(2)}) collective-permute-start(f32[128,3,1,128]{3,2,0,1:T(1,128)S(1)} %get-tuple-element.8), channel_id=1, source_target_pairs={{1,2},{5,6},{7,8},{9,10},{13,14},{2,1},{6,5},{8,7},{10,9},{14,13},... | collective-permute-start | bytes 589832 | tf_op jit(solution)/shard_map/ppermute | solution.py:28
  194.1 4.4 %collective-permute-done.16 = f32[128,3,1,128]{3,2,0,1:T(1,128)S(1)} collective-permute-done((f32[128,3,1,128]{3,2,0,1:T(1,128)S(1)}, f32[128,3,1,128]{3,2,0,1:T(1,128)S(1)}, u32[]{:S(2)}, u32[]{:S(2)}) %collective-permute-start.16) | collective-permute-done | bytes 196640 | tf_op jit(solution)/shard_map/ppermute | solution.py:28
  198.5 1.2 maximum_multiply_fusion
  199.9 0.5 pad_maximum_fusion
  200.4 1.6 fusion.82
  202.0 1.9 fusion.8
  203.9 1.9 copy.51
  205.8 3.5 %fusion.196 = f32[16,16,4096]{2,1,0:T(8,128)S(1)} fusion(f32[128,4096,1]{0,1,2:T(8,128)} %bitcast.205, s32[16,16]{1,0:T(8,128)S(1)} %multiply_add_fusion.1, s32[128]{0:T(128)S(1)} %get-tuple-element.102), kind=kOutput, calls=%fused_computation.324 | convolution fusion | flops 1610645504 | bytes 6292992 | tf_op jit(solution)/shard_map/dot_general | solution.py:212
  209.3 97.7 %all_to_all.20 = f32[16,16,4096]{2,1,0:T(8,128)S(1)} all-to-all(f32[16,16,4096]{2,1,0:T(8,128)S(1)} %fusion.196), channel_id=1, replica_groups=mesh['groups'=2,'shot'=16] {'shot'}, dimensions={0} | all-to-all | bytes 8388608 | tf_op jit(solution)/shard_map/all_to_all | solution.py:213
  307.0 1.8 convolution_multiply_fusion
  308.8 1.9 reshape.268
  (92 shorter events, 6.5 us)
Async XLA Ops:
  20.8 7.2 %copy-start = (f32[128,16,128]{2,1,0:T(8,128)S(1)}, f32[128,16,128]{2,1,0:T(8,128)}, u32[]{:S(2)}) copy-start(f32[128,16,128]{2,1,0:T(8,128)} %param.16) | copy-start | bytes 3145732
  20.8 16.3 %copy-start.6 = (f32[1,4]{1,0:T(1,128)S(1)}, f32[1,4]{1,0:T(1,128)}, u32[]{:S(2)}) copy-start(f32[1,4]{1,0:T(1,128)} %param.21) | copy-start | bytes 52
  20.8 16.9 %copy-start.8 = (s32[1,256]{1,0:T(1,128)S(1)}, s32[1,256]{1,0:T(1,128)}, u32[]{:S(2)}) copy-start(s32[1,256]{1,0:T(1,128)} %param.22) | copy-start | bytes 3076
  20.8 16.9 %copy-start.7 = (f32[1,4,256]{2,1,0:T(4,128)S(1)}, f32[1,4,256]{2,1,0:T(4,128)}, u32[]{:S(2)}) copy-start(f32[1,4,256]{2,1,0:T(4,128)} %param.23) | copy-start | bytes 12292
  20.8 101.6 %all-to-all-start.1 = ((f32[16,16,4096]{2,1,0:T(8,128)}), f32[16,16,4096]{2,1,0:T(8,128)}, u32[]{:S(2)}, u32[]{:S(2)}) async-start(f32[16,16,4096]{2,1,0:T(8,128)} %bitcast.199), calls=%async_computation.1 | async-start | bytes 8388608 | tf_op jit(solution)/shard_map/all_to_all | solution.py:143
  28.0 93.0 %collective-permute-start = (f32[128,1,128]{2,1,0:T(1,128)S(1)}, f32[128,1,128]{2,1,0:T(1,128)S(1)}, u32[]{:S(2)}, u32[]{:S(2)}) collective-permute-start(f32[128,1,128]{2,1,0:T(1,128)S(1)} %get-tuple-element.55), channel_id=1, source_target_pairs={{1,2},{5,6},{7,8},{9,10},{13,14},{2,1},{6,5},{8,7},{10,9},{14,13},... | collective-permute-start | bytes 196616 | tf_op jit(solution)/shard_map/ppermute | solution.py:28
  31.4 89.6 %collective-permute-start.1 = (f32[128,1,128]{2,1,0:T(1,128)S(1)}, f32[128,1,128]{2,1,0:T(1,128)S(1)}, u32[]{:S(2)}, u32[]{:S(2)}) collective-permute-start(f32[128,1,128]{2,1,0:T(1,128)S(1)} %get-tuple-element.56), channel_id=1, source_target_pairs={{0,1},{2,3},{4,5},{6,7},{8,9},{10,11},{12,13},{14,15},{1,0},{3,2},... | collective-permute-start | bytes 196616 | tf_op jit(solution)/shard_map/ppermute | solution.py:27
  32.8 89.6 %collective-permute-start.8 = (f32[128,1,128]{2,1,0:T(1,128)S(1)}, f32[128,1,128]{2,1,0:T(1,128)S(1)}, u32[]{:S(2)}, u32[]{:S(2)}) collective-permute-start(f32[128,1,128]{2,1,0:T(1,128)S(1)} %get-tuple-element.35), channel_id=1, source_target_pairs={{1,2},{5,6},{7,8},{9,10},{13,14},{2,1},{6,5},{8,7},{10,9},{14,13},... | collective-permute-start | bytes 196616 | tf_op jit(solution)/shard_map/ppermute | solution.py:28
  36.2 86.1 %collective-permute-start.9 = (f32[128,1,128]{2,1,0:T(1,128)S(1)}, f32[128,1,128]{2,1,0:T(1,128)S(1)}, u32[]{:S(2)}, u32[]{:S(2)}) collective-permute-start(f32[128,1,128]{2,1,0:T(1,128)S(1)} %get-tuple-element.36), channel_id=1, source_target_pairs={{0,1},{2,3},{4,5},{6,7},{8,9},{10,11},{12,13},{14,15},{1,0},{3,2},... | collective-permute-start | bytes 196616 | tf_op jit(solution)/shard_map/ppermute | solution.py:27
  126.5 1.2 copy-start.2
  126.5 1.5 copy-start.4
  130.5 6.5 %collective-permute-start.2 = (f32[128,1,128]{2,1,0:T(1,128)S(1)}, f32[128,1,128]{2,1,0:T(1,128)S(1)}, u32[]{:S(2)}, u32[]{:S(2)}) collective-permute-start(f32[128,1,128]{2,1,0:T(1,128)S(1)} %get-tuple-element.53), channel_id=1, source_target_pairs={{1,2},{5,6},{7,8},{9,10},{13,14},{2,1},{6,5},{8,7},{10,9},{14,13},... | collective-permute-start | bytes 196616 | tf_op jit(solution)/shard_map/ppermute | solution.py:28
  134.0 2.9 collective-permute-start.3
  134.1 2.9 copy-start.1
  140.1 6.5 %collective-permute-start.4 = (f32[128,1,128]{2,1,0:T(1,128)S(1)}, f32[128,1,128]{2,1,0:T(1,128)S(1)}, u32[]{:S(2)}, u32[]{:S(2)}) collective-permute-start(f32[128,1,128]{2,1,0:T(1,128)S(1)} %get-tuple-element.51), channel_id=1, source_target_pairs={{1,2},{5,6},{7,8},{9,10},{13,14},{2,1},{6,5},{8,7},{10,9},{14,13},... | collective-permute-start | bytes 196616 | tf_op jit(solution)/shard_map/ppermute | solution.py:28
  143.9 2.7 collective-permute-start.5
  149.6 6.5 %collective-permute-start.6 = (f32[128,1,128]{2,1,0:T(1,128)S(1)}, f32[128,1,128]{2,1,0:T(1,128)S(1)}, u32[]{:S(2)}, u32[]{:S(2)}) collective-permute-start(f32[128,1,128]{2,1,0:T(1,128)S(1)} %get-tuple-element.49), channel_id=1, source_target_pairs={{1,2},{5,6},{7,8},{9,10},{13,14},{2,1},{6,5},{8,7},{10,9},{14,13},... | collective-permute-start | bytes 196616 | tf_op jit(solution)/shard_map/ppermute | solution.py:28
  153.1 2.9 collective-permute-start.7
  158.6 1.1 copy-start.3
  161.0 1.2 copy-start.5
  163.4 6.5 %collective-permute-start.10 = (f32[128,1,128]{2,1,0:T(1,128)S(1)}, f32[128,1,128]{2,1,0:T(1,128)S(1)}, u32[]{:S(2)}, u32[]{:S(2)}) collective-permute-start(f32[128,1,128]{2,1,0:T(1,128)S(1)} %get-tuple-element.33), channel_id=1, source_target_pairs={{1,2},{5,6},{7,8},{9,10},{13,14},{2,1},{6,5},{8,7},{10,9},{14,13},... | collective-permute-start | bytes 196616 | tf_op jit(solution)/shard_map/ppermute | solution.py:28
  166.9 2.9 collective-permute-start.11
  171.4 6.5 %collective-permute-start.12 = (f32[128,1,128]{2,1,0:T(1,128)S(1)}, f32[128,1,128]{2,1,0:T(1,128)S(1)}, u32[]{:S(2)}, u32[]{:S(2)}) collective-permute-start(f32[128,1,128]{2,1,0:T(1,128)S(1)} %get-tuple-element.31), channel_id=1, source_target_pairs={{1,2},{5,6},{7,8},{9,10},{13,14},{2,1},{6,5},{8,7},{10,9},{14,13},... | collective-permute-start | bytes 196616 | tf_op jit(solution)/shard_map/ppermute | solution.py:28
  175.2 2.7 collective-permute-start.13
  179.3 6.5 %collective-permute-start.14 = (f32[128,1,128]{2,1,0:T(1,128)S(1)}, f32[128,1,128]{2,1,0:T(1,128)S(1)}, u32[]{:S(2)}, u32[]{:S(2)}) collective-permute-start(f32[128,1,128]{2,1,0:T(1,128)S(1)} %get-tuple-element.29), channel_id=1, source_target_pairs={{1,2},{5,6},{7,8},{9,10},{13,14},{2,1},{6,5},{8,7},{10,9},{14,13},... | collective-permute-start | bytes 196616 | tf_op jit(solution)/shard_map/ppermute | solution.py:28
  182.8 2.9 collective-permute-start.15
  190.4 3.7 %collective-permute-start.17 = (f32[128,3,1,128]{3,2,0,1:T(1,128)S(1)}, f32[128,3,1,128]{3,2,0,1:T(1,128)S(1)}, u32[]{:S(2)}, u32[]{:S(2)}) collective-permute-start(f32[128,3,1,128]{3,2,0,1:T(1,128)S(1)} %bitcast.232), channel_id=1, source_target_pairs={{0,1},{2,3},{4,5},{6,7},{8,9},{10,11},{12,13},{14,15},{1,0},{3,2},... | collective-permute-start | bytes 589832 | tf_op jit(solution)/shard_map/ppermute | solution.py:27
  190.5 8.0 %collective-permute-start.16 = (f32[128,3,1,128]{3,2,0,1:T(1,128)S(1)}, f32[128,3,1,128]{3,2,0,1:T(1,128)S(1)}, u32[]{:S(2)}, u32[]{:S(2)}) collective-permute-start(f32[128,3,1,128]{3,2,0,1:T(1,128)S(1)} %get-tuple-element.8), channel_id=1, source_target_pairs={{1,2},{5,6},{7,8},{9,10},{13,14},{2,1},{6,5},{8,7},{10,9},{14,13},... | collective-permute-start | bytes 589832 | tf_op jit(solution)/shard_map/ppermute | solution.py:28

commit v3 on v2

--- a/solution.py
+++ b/solution.py
@@ -45,15 +45,15 @@
 
 
 def forward_rims(wavefield):
-    return cross_mask(extended(wavefield, (("shot", 1),), 1), 1)
+    return extended(wavefield, (("shot", 1),), 1)
 
 
 def adjoint_rims_of(wavefield):
-    return cross_mask(extended(wavefield, (("shot", 1),), 1), 1)
+    return extended(wavefield, (("shot", 1),), 1)
 
 
 def image_rims_of(stacked):
-    return cross_mask(extended(stacked, (("shot", 2),), 1), 2)
+    return extended(stacked, (("shot", 2),), 1)
 
 
 def curvatures(widened):

time: 313 us -> 316 us (level)
  starting transfers between devices: 39.9 us -> 44.1 us
    add x4, other arithmetic: 8.35 us -> 14.3 us  [shards(): advanced = advanced + jnp.where(at_source, wavelet[0, time_step], 0.0)]
    ppermute x9, starting transfers between devices: 32.1 us -> 36 us  [extended(): got_outer = lax.ppermute(jnp.where(even, leading, last), axis, outer)]
    mul x8 -> x0, other arithmetic: 3.47 us -> none  [cross_mask(): return widened * keep_mask.reshape(dims_out)]
  transfers between devices with their start and end apart: 19 -> 19, of which waited for: 8 -> 9; matrix products, arithmetic and copies ran while one was open for 3% -> 2% of each run, Pallas kernels for 0% -> 0%
where the time goes in v3:
time: 316 us; the launch traced here: 314 us
  blocking collectives  109 us (34%)
  waiting for transfers between devices  97.6 us (31%)
  starting transfers between devices  44.1 us (14%)
  other arithmetic  32.5 us (10%)
  matrix products  20.1 us (6%)
  local copies, waits for them, and re-layouts  8.68 us (3%)
    all_to_all x1, blocking collectives, shards(): lax.all_to_all(returning.reshape(shot_count, capacity, 2 * row_len), 'sho...  98.7 us
    ppermute x9, waiting for transfers between devices, extended(): got_outer = lax.ppermute(jnp.where(even, leading, last), axis, outer)  97.6 us
    ppermute x9, starting transfers between devices, extended(): got_outer = lax.ppermute(jnp.where(even, leading, last), axis, outer)  36 us
    add x4, other arithmetic, shards(): advanced = advanced + jnp.where(at_source, wavelet[0, time_step], 0.0)  14.3 us
    all_to_all x1, blocking collectives, shards(): lax.all_to_all(requests.reshape(shot_count, capacity), 'shot', split_axis...  10.2 us
    all_to_all x1, starting transfers between devices, shards(): lax.all_to_all(outgoing.reshape(shot_count, capacity, 2 * row_len), 'shot...  7.15 us
  transfers between devices with their start and end apart: 19, of which 9 were waited for; matrix products, arithmetic and copies ran while one was open for 2% of the time, Pallas kernels for 0%

profile of v3, /device:TPU:13, one launch (start us, length us, event | category | flops | bytes accessed | tf_op | source)
XLA Modules:
  0.0 313.9 jit_solution(2176605704823190841)
XLA Ops:
  0.6 0.7 fusion.213
  1.5 0.8 select_reduce_fusion
  2.4 0.7 fusion.226
  3.0 1.1 scatter_custom_fusion
  4.2 10.2 %all_to_all.19 = s32[16,1,16]{2,1,0:T(1,128)S(1)} all-to-all(s32[16,1,16]{2,1,0:T(1,128)S(1)} %all_to_all.12), channel_id=1, replica_groups=mesh['groups'=2,'shot'=16] {'shot'}, dimensions={0} | all-to-all | bytes 2048 | tf_op jit(solution)/shard_map/all_to_all | solution.py:134
  14.4 0.5 broadcast.311
  14.9 0.7 reduce.3
  15.7 5.1 %fusion.159 = f32[256,4096]{1,0:T(8,128)} fusion(f32[64,2048]{1,0:T(8,128)} %param.13, f32[64,2048]{1,0:T(8,128)} %param.12, s32[256]{0:T(256)S(1)} %eq.166), kind=kOutput, calls=%fused_computation.258 | convolution fusion | flops 805584896 | bytes 5243904 | tf_op jit(solution)/shard_map/dot_general | solution.py:142
  20.8 7.2 %all-to-all-start.1 = ((f32[16,16,4096]{2,1,0:T(8,128)}), f32[16,16,4096]{2,1,0:T(8,128)}, u32[]{:S(2)}, u32[]{:S(2)}) async-start(f32[16,16,4096]{2,1,0:T(8,128)} %bitcast.243), calls=%async_computation.1 | async-start | bytes 8388608 | tf_op jit(solution)/shard_map/all_to_all | solution.py:143
  28.0 0.4 collective-permute-start
  28.5 3.1 collective-permute-start.1
  31.8 3.5 %collective-permute-start.9 = (f32[128,1,128]{2,1,0:T(1,128)S(1)}, f32[128,1,128]{2,1,0:T(1,128)S(1)}, u32[]{:S(2)}, u32[]{:S(2)}) collective-permute-start(f32[128,1,128]{2,1,0:T(1,128)S(1)} %get-tuple-element.37), channel_id=1, source_target_pairs={{1,2},{5,6},{7,8},{9,10},{13,14},{2,1},{6,5},{8,7},{10,9},{14,13},... | collective-permute-start | bytes 196616 | tf_op jit(solution)/shard_map/ppermute | solution.py:28
  36.0 0.6 fusion.235
  36.7 84.3 %collective-permute-done.1 = f32[128,1,128]{2,1,0:T(1,128)S(1)} collective-permute-done((f32[128,1,128]{2,1,0:T(1,128)S(1)}, f32[128,1,128]{2,1,0:T(1,128)S(1)}, u32[]{:S(2)}, u32[]{:S(2)}) %collective-permute-start.1) | collective-permute-done | bytes 65568 | tf_op jit(solution)/shard_map/ppermute | solution.py:28
  121.0 0.7 collective-permute-done.9
  121.7 3.9 %fusion.205 = f32[128,4096]{1,0:T(8,128)S(1)} fusion(f32[256,4096]{1,0:T(8,128)} %bitcast.5, s32[128]{0:T(128)S(1)} %get-tuple-element.103), kind=kOutput, calls=%fused_computation.341 | convolution fusion | flops 1610645504 | bytes 6291968 | tf_op jit(solution)/shard_map/dot_general | solution.py:153
  126.2 0.8 copy-done.1
  127.0 2.1 fusion.108
  129.2 0.3 reduce-precision_convert_fusion.1
  129.6 3.6 %collective-permute-start.3 = (f32[128,1,128]{2,1,0:T(1,128)S(1)}, f32[128,1,128]{2,1,0:T(1,128)S(1)}, u32[]{:S(2)}, u32[]{:S(2)}) collective-permute-start(f32[128,1,128]{2,1,0:T(1,128)S(1)} %get-tuple-element.55), channel_id=1, source_target_pairs={{1,2},{5,6},{7,8},{9,10},{13,14},{2,1},{6,5},{8,7},{10,9},{14,13},... | collective-permute-start | bytes 196616 | tf_op jit(solution)/shard_map/ppermute | solution.py:28
  133.1 0.8 fusion.23
  133.9 2.2 collective-permute-done.3
  136.1 3.0 fusion.112
  139.2 0.3 reduce-precision_convert_fusion.3
  139.6 3.8 %collective-permute-start.5 = (f32[128,1,128]{2,1,0:T(1,128)S(1)}, f32[128,1,128]{2,1,0:T(1,128)S(1)}, u32[]{:S(2)}, u32[]{:S(2)}) collective-permute-start(f32[128,1,128]{2,1,0:T(1,128)S(1)} %get-tuple-element.53), channel_id=1, source_target_pairs={{1,2},{5,6},{7,8},{9,10},{13,14},{2,1},{6,5},{8,7},{10,9},{14,13},... | collective-permute-start | bytes 196616 | tf_op jit(solution)/shard_map/ppermute | solution.py:28
  143.4 0.8 fusion.24
  144.2 1.9 collective-permute-done.5
  146.1 4.2 %fusion.116 = (f32[128,16,128]{2,1,0:T(8,128)S(1)}, f32[128,16,128]{2,1,0:T(8,128)S(1)}, f32[128,16,128]{2,1,0:T(8,128)S(1)}) fusion(f32[16,8,16,128]{3,2,1,0:T(8,128)S(1)} %copy.70, f32[16,8,16,128]{3,2,1,0:T(8,128)S(1)} %copy.69, f32[128,16,128]{2,1,0:T(8,128)S(1)} %get-tuple-element.18, f32[128,16,128]{2,1,0:T(8,128)S(1)} %get-tuple-element.17, ...), kind=kLoop, calls=%fused_computation.186 | loop fusion | flops 9699328 | bytes 12714576 | tf_op jit(solution)/shard_map/add | solution.py:177
  150.3 0.3 reduce-precision_convert_fusion.5
  150.7 4.1 %collective-permute-start.7 = (f32[128,1,128]{2,1,0:T(1,128)S(1)}, f32[128,1,128]{2,1,0:T(1,128)S(1)}, u32[]{:S(2)}, u32[]{:S(2)}) collective-permute-start(f32[128,1,128]{2,1,0:T(1,128)S(1)} %get-tuple-element.51), channel_id=1, source_target_pairs={{1,2},{5,6},{7,8},{9,10},{13,14},{2,1},{6,5},{8,7},{10,9},{14,13},... | collective-permute-start | bytes 196616 | tf_op jit(solution)/shard_map/ppermute | solution.py:28
  154.8 0.8 fusion.25
  155.6 1.6 collective-permute-done.7
  157.2 5.0 %fusion.120 = (f32[128,16,128]{2,1,0:T(8,128)S(1)}, f32[128,16,128]{2,1,0:T(8,128)S(1)}) fusion(f32[16,8,16,128]{3,2,1,0:T(8,128)S(1)} %copy.70, f32[16,8,16,128]{3,2,1,0:T(8,128)S(1)} %copy.69, f32[128,16,128]{2,1,0:T(8,128)S(1)} %get-tuple-element.15, f32[128,16,128]{2,1,0:T(8,128)S(1)} %get-tuple-element.14, f32[128,16,128]{2,1,0:T(8,128)S(1)} %get-tuple-element.18, ...), kind=kLoop, calls=%fused_computation.190 | loop fusion | flops 11796480 | bytes 13763156 | tf_op jit(solution)/shard_map/add | solution.py:177
  162.2 0.3 reduce-precision_convert_fusion.7
  162.5 0.8 fusion.26
  163.3 0.3 fusion.198
  163.7 0.3 reduce-precision_convert_fusion.9
  163.9 0.7 fusion.22
  164.8 1.1 copy-done.4
  165.9 0.9 fusion.64
  167.0 4.2 %collective-permute-start.11 = (f32[128,1,128]{2,1,0:T(1,128)S(1)}, f32[128,1,128]{2,1,0:T(1,128)S(1)}, u32[]{:S(2)}, u32[]{:S(2)}) collective-permute-start(f32[128,1,128]{2,1,0:T(1,128)S(1)} %get-tuple-element.35), channel_id=1, source_target_pairs={{1,2},{5,6},{7,8},{9,10},{13,14},{2,1},{6,5},{8,7},{10,9},{14,13},... | collective-permute-start | bytes 196616 | tf_op jit(solution)/shard_map/ppermute | solution.py:28
  171.2 0.7 fusion.21
  172.0 0.7 fusion.20
  172.9 0.6 collective-permute-done.11
  173.5 0.9 fusion.70
  174.6 4.3 %collective-permute-start.13 = (f32[128,1,128]{2,1,0:T(1,128)S(1)}, f32[128,1,128]{2,1,0:T(1,128)S(1)}, u32[]{:S(2)}, u32[]{:S(2)}) collective-permute-start(f32[128,1,128]{2,1,0:T(1,128)S(1)} %get-tuple-element.33), channel_id=1, source_target_pairs={{1,2},{5,6},{7,8},{9,10},{13,14},{2,1},{6,5},{8,7},{10,9},{14,13},... | collective-permute-start | bytes 196616 | tf_op jit(solution)/shard_map/ppermute | solution.py:28
  178.9 0.7 fusion.19
  179.6 1.5 collective-permute-done.13
  181.1 0.8 fusion.76
  182.1 4.8 %collective-permute-start.15 = (f32[128,1,128]{2,1,0:T(1,128)S(1)}, f32[128,1,128]{2,1,0:T(1,128)S(1)}, u32[]{:S(2)}, u32[]{:S(2)}) collective-permute-start(f32[128,1,128]{2,1,0:T(1,128)S(1)} %get-tuple-element.31), channel_id=1, source_target_pairs={{1,2},{5,6},{7,8},{9,10},{13,14},{2,1},{6,5},{8,7},{10,9},{14,13},... | collective-permute-start | bytes 196616 | tf_op jit(solution)/shard_map/ppermute | solution.py:28
  187.0 1.6 collective-permute-done.15
  188.6 2.3 fusion.121
  191.0 1.1 fusion.122
  192.1 0.3 broadcast_select_fusion.3
  192.6 4.6 %collective-permute-start.16 = (f32[128,3,1,128]{3,2,0,1:T(1,128)S(1)}, f32[128,3,1,128]{3,2,0,1:T(1,128)S(1)}, u32[]{:S(2)}, u32[]{:S(2)}) collective-permute-start(f32[128,3,1,128]{3,2,0,1:T(1,128)S(1)} %get-tuple-element.8), channel_id=1, source_target_pairs={{1,2},{5,6},{7,8},{9,10},{13,14},{2,1},{6,5},{8,7},{10,9},{14,13},... | collective-permute-start | bytes 589832 | tf_op jit(solution)/shard_map/ppermute | solution.py:28
  197.3 3.4 %collective-permute-done.16 = f32[128,3,1,128]{3,2,0,1:T(1,128)S(1)} collective-permute-done((f32[128,3,1,128]{3,2,0,1:T(1,128)S(1)}, f32[128,3,1,128]{3,2,0,1:T(1,128)S(1)}, u32[]{:S(2)}, u32[]{:S(2)}) %collective-permute-start.16) | collective-permute-done | bytes 196640 | tf_op jit(solution)/shard_map/ppermute | solution.py:28
  200.9 0.6 pad_maximum_fusion
  201.5 2.0 fusion.84
  203.5 2.7 fusion.8
  206.2 1.9 copy.65
  208.1 3.5 %fusion.206 = f32[16,16,4096]{2,1,0:T(8,128)S(1)} fusion(f32[128,4096,1]{0,1,2:T(8,128)} %bitcast.247, s32[16,16]{1,0:T(8,128)S(1)} %multiply_add_fusion.2, s32[128]{0:T(128)S(1)} %get-tuple-element.103), kind=kOutput, calls=%fused_computation.342 | convolution fusion | flops 1610645504 | bytes 6292992 | tf_op jit(solution)/shard_map/dot_general | solution.py:212
  211.6 98.7 %all_to_all.20 = f32[16,16,4096]{2,1,0:T(8,128)S(1)} all-to-all(f32[16,16,4096]{2,1,0:T(8,128)S(1)} %fusion.206), channel_id=1, replica_groups=mesh['groups'=2,'shot'=16] {'shot'}, dimensions={0} | all-to-all | bytes 8388608 | tf_op jit(solution)/shard_map/all_to_all | solution.py:213
  310.3 1.8 convolution_multiply_fusion
  312.1 1.9 reshape.239
  (73 shorter events, 3.3 us)
Async XLA Ops:
  20.8 7.2 %copy-start = (f32[128,16,128]{2,1,0:T(8,128)S(1)}, f32[128,16,128]{2,1,0:T(8,128)}, u32[]{:S(2)}) copy-start(f32[128,16,128]{2,1,0:T(8,128)} %param.16) | copy-start | bytes 3145732
  20.8 10.9 %copy-start.2 = (f32[128,16,128]{2,1,0:T(8,128)S(1)}, f32[128,16,128]{2,1,0:T(8,128)}, u32[]{:S(2)}) copy-start(f32[128,16,128]{2,1,0:T(8,128)} %param.18) | copy-start | bytes 3145732
  20.8 15.2 %copy-start.5 = (f32[1,4]{1,0:T(1,128)S(1)}, f32[1,4]{1,0:T(1,128)}, u32[]{:S(2)}) copy-start(f32[1,4]{1,0:T(1,128)} %param.21) | copy-start | bytes 52
  20.8 15.8 %copy-start.7 = (s32[1,256]{1,0:T(1,128)S(1)}, s32[1,256]{1,0:T(1,128)}, u32[]{:S(2)}) copy-start(s32[1,256]{1,0:T(1,128)} %param.22) | copy-start | bytes 3076
  20.8 15.9 %copy-start.6 = (f32[1,4,256]{2,1,0:T(4,128)S(1)}, f32[1,4,256]{2,1,0:T(4,128)}, u32[]{:S(2)}) copy-start(f32[1,4,256]{2,1,0:T(4,128)} %param.23) | copy-start | bytes 12292
  20.8 100.9 %all-to-all-start.1 = ((f32[16,16,4096]{2,1,0:T(8,128)}), f32[16,16,4096]{2,1,0:T(8,128)}, u32[]{:S(2)}, u32[]{:S(2)}) async-start(f32[16,16,4096]{2,1,0:T(8,128)} %bitcast.243), calls=%async_computation.1 | async-start | bytes 8388608 | tf_op jit(solution)/shard_map/all_to_all | solution.py:143
  28.0 8.6 %collective-permute-start = (f32[128,1,128]{2,1,0:T(1,128)S(1)}, f32[128,1,128]{2,1,0:T(1,128)S(1)}, u32[]{:S(2)}, u32[]{:S(2)}) collective-permute-start(f32[128,1,128]{2,1,0:T(1,128)S(1)} %get-tuple-element.56), channel_id=1, source_target_pairs={{0,1},{2,3},{4,5},{6,7},{8,9},{10,11},{12,13},{14,15},{1,0},{3,2},... | collective-permute-start | bytes 196616 | tf_op jit(solution)/shard_map/ppermute | solution.py:27
  28.5 92.5 %collective-permute-start.1 = (f32[128,1,128]{2,1,0:T(1,128)S(1)}, f32[128,1,128]{2,1,0:T(1,128)S(1)}, u32[]{:S(2)}, u32[]{:S(2)}) collective-permute-start(f32[128,1,128]{2,1,0:T(1,128)S(1)} %get-tuple-element.57), channel_id=1, source_target_pairs={{1,2},{5,6},{7,8},{9,10},{13,14},{2,1},{6,5},{8,7},{10,9},{14,13},... | collective-permute-start | bytes 196616 | tf_op jit(solution)/shard_map/ppermute | solution.py:28
  31.7 89.3 %collective-permute-start.8 = (f32[128,1,128]{2,1,0:T(1,128)S(1)}, f32[128,1,128]{2,1,0:T(1,128)S(1)}, u32[]{:S(2)}, u32[]{:S(2)}) collective-permute-start(f32[128,1,128]{2,1,0:T(1,128)S(1)} %get-tuple-element.36), channel_id=1, source_target_pairs={{0,1},{2,3},{4,5},{6,7},{8,9},{10,11},{12,13},{14,15},{1,0},{3,2},... | collective-permute-start | bytes 196616 | tf_op jit(solution)/shard_map/ppermute | solution.py:27
  31.8 89.9 %collective-permute-start.9 = (f32[128,1,128]{2,1,0:T(1,128)S(1)}, f32[128,1,128]{2,1,0:T(1,128)S(1)}, u32[]{:S(2)}, u32[]{:S(2)}) collective-permute-start(f32[128,1,128]{2,1,0:T(1,128)S(1)} %get-tuple-element.37), channel_id=1, source_target_pairs={{1,2},{5,6},{7,8},{9,10},{13,14},{2,1},{6,5},{8,7},{10,9},{14,13},... | collective-permute-start | bytes 196616 | tf_op jit(solution)/shard_map/ppermute | solution.py:28
  125.8 1.2 copy-start.1
  129.5 4.4 %collective-permute-start.2 = (f32[128,1,128]{2,1,0:T(1,128)S(1)}, f32[128,1,128]{2,1,0:T(1,128)S(1)}, u32[]{:S(2)}, u32[]{:S(2)}) collective-permute-start(f32[128,1,128]{2,1,0:T(1,128)S(1)} %get-tuple-element.54), channel_id=1, source_target_pairs={{0,1},{2,3},{4,5},{6,7},{8,9},{10,11},{12,13},{14,15},{1,0},{3,2},... | collective-permute-start | bytes 196616 | tf_op jit(solution)/shard_map/ppermute | solution.py:27
  129.6 6.5 %collective-permute-start.3 = (f32[128,1,128]{2,1,0:T(1,128)S(1)}, f32[128,1,128]{2,1,0:T(1,128)S(1)}, u32[]{:S(2)}, u32[]{:S(2)}) collective-permute-start(f32[128,1,128]{2,1,0:T(1,128)S(1)} %get-tuple-element.55), channel_id=1, source_target_pairs={{1,2},{5,6},{7,8},{9,10},{13,14},{2,1},{6,5},{8,7},{10,9},{14,13},... | collective-permute-start | bytes 196616 | tf_op jit(solution)/shard_map/ppermute | solution.py:28
  139.5 4.7 %collective-permute-start.4 = (f32[128,1,128]{2,1,0:T(1,128)S(1)}, f32[128,1,128]{2,1,0:T(1,128)S(1)}, u32[]{:S(2)}, u32[]{:S(2)}) collective-permute-start(f32[128,1,128]{2,1,0:T(1,128)S(1)} %get-tuple-element.52), channel_id=1, source_target_pairs={{0,1},{2,3},{4,5},{6,7},{8,9},{10,11},{12,13},{14,15},{1,0},{3,2},... | collective-permute-start | bytes 196616 | tf_op jit(solution)/shard_map/ppermute | solution.py:27
  139.6 6.5 %collective-permute-start.5 = (f32[128,1,128]{2,1,0:T(1,128)S(1)}, f32[128,1,128]{2,1,0:T(1,128)S(1)}, u32[]{:S(2)}, u32[]{:S(2)}) collective-permute-start(f32[128,1,128]{2,1,0:T(1,128)S(1)} %get-tuple-element.53), channel_id=1, source_target_pairs={{1,2},{5,6},{7,8},{9,10},{13,14},{2,1},{6,5},{8,7},{10,9},{14,13},... | collective-permute-start | bytes 196616 | tf_op jit(solution)/shard_map/ppermute | solution.py:28
  150.6 5.0 %collective-permute-start.6 = (f32[128,1,128]{2,1,0:T(1,128)S(1)}, f32[128,1,128]{2,1,0:T(1,128)S(1)}, u32[]{:S(2)}, u32[]{:S(2)}) collective-permute-start(f32[128,1,128]{2,1,0:T(1,128)S(1)} %get-tuple-element.50), channel_id=1, source_target_pairs={{0,1},{2,3},{4,5},{6,7},{8,9},{10,11},{12,13},{14,15},{1,0},{3,2},... | collective-permute-start | bytes 196616 | tf_op jit(solution)/shard_map/ppermute | solution.py:27
  150.7 6.5 %collective-permute-start.7 = (f32[128,1,128]{2,1,0:T(1,128)S(1)}, f32[128,1,128]{2,1,0:T(1,128)S(1)}, u32[]{:S(2)}, u32[]{:S(2)}) collective-permute-start(f32[128,1,128]{2,1,0:T(1,128)S(1)} %get-tuple-element.51), channel_id=1, source_target_pairs={{1,2},{5,6},{7,8},{9,10},{13,14},{2,1},{6,5},{8,7},{10,9},{14,13},... | collective-permute-start | bytes 196616 | tf_op jit(solution)/shard_map/ppermute | solution.py:28
  162.2 1.1 copy-start.3
  164.6 1.2 copy-start.4
  166.9 6.0 %collective-permute-start.10 = (f32[128,1,128]{2,1,0:T(1,128)S(1)}, f32[128,1,128]{2,1,0:T(1,128)S(1)}, u32[]{:S(2)}, u32[]{:S(2)}) collective-permute-start(f32[128,1,128]{2,1,0:T(1,128)S(1)} %get-tuple-element.34), channel_id=1, source_target_pairs={{0,1},{2,3},{4,5},{6,7},{8,9},{10,11},{12,13},{14,15},{1,0},{3,2},... | collective-permute-start | bytes 196616 | tf_op jit(solution)/shard_map/ppermute | solution.py:27
  167.0 6.5 %collective-permute-start.11 = (f32[128,1,128]{2,1,0:T(1,128)S(1)}, f32[128,1,128]{2,1,0:T(1,128)S(1)}, u32[]{:S(2)}, u32[]{:S(2)}) collective-permute-start(f32[128,1,128]{2,1,0:T(1,128)S(1)} %get-tuple-element.35), channel_id=1, source_target_pairs={{1,2},{5,6},{7,8},{9,10},{13,14},{2,1},{6,5},{8,7},{10,9},{14,13},... | collective-permute-start | bytes 196616 | tf_op jit(solution)/shard_map/ppermute | solution.py:28
  174.5 5.1 %collective-permute-start.12 = (f32[128,1,128]{2,1,0:T(1,128)S(1)}, f32[128,1,128]{2,1,0:T(1,128)S(1)}, u32[]{:S(2)}, u32[]{:S(2)}) collective-permute-start(f32[128,1,128]{2,1,0:T(1,128)S(1)} %get-tuple-element.32), channel_id=1, source_target_pairs={{0,1},{2,3},{4,5},{6,7},{8,9},{10,11},{12,13},{14,15},{1,0},{3,2},... | collective-permute-start | bytes 196616 | tf_op jit(solution)/shard_map/ppermute | solution.py:27
  174.6 6.5 %collective-permute-start.13 = (f32[128,1,128]{2,1,0:T(1,128)S(1)}, f32[128,1,128]{2,1,0:T(1,128)S(1)}, u32[]{:S(2)}, u32[]{:S(2)}) collective-permute-start(f32[128,1,128]{2,1,0:T(1,128)S(1)} %get-tuple-element.33), channel_id=1, source_target_pairs={{1,2},{5,6},{7,8},{9,10},{13,14},{2,1},{6,5},{8,7},{10,9},{14,13},... | collective-permute-start | bytes 196616 | tf_op jit(solution)/shard_map/ppermute | solution.py:28
  182.0 5.0 %collective-permute-start.14 = (f32[128,1,128]{2,1,0:T(1,128)S(1)}, f32[128,1,128]{2,1,0:T(1,128)S(1)}, u32[]{:S(2)}, u32[]{:S(2)}) collective-permute-start(f32[128,1,128]{2,1,0:T(1,128)S(1)} %get-tuple-element.30), channel_id=1, source_target_pairs={{0,1},{2,3},{4,5},{6,7},{8,9},{10,11},{12,13},{14,15},{1,0},{3,2},... | collective-permute-start | bytes 196616 | tf_op jit(solution)/shard_map/ppermute | solution.py:27
  182.1 6.5 %collective-permute-start.15 = (f32[128,1,128]{2,1,0:T(1,128)S(1)}, f32[128,1,128]{2,1,0:T(1,128)S(1)}, u32[]{:S(2)}, u32[]{:S(2)}) collective-permute-start(f32[128,1,128]{2,1,0:T(1,128)S(1)} %get-tuple-element.31), channel_id=1, source_target_pairs={{1,2},{5,6},{7,8},{9,10},{13,14},{2,1},{6,5},{8,7},{10,9},{14,13},... | collective-permute-start | bytes 196616 | tf_op jit(solution)/shard_map/ppermute | solution.py:28
  192.5 4.8 %collective-permute-start.17 = (f32[128,3,1,128]{3,2,0,1:T(1,128)S(1)}, f32[128,3,1,128]{3,2,0,1:T(1,128)S(1)}, u32[]{:S(2)}, u32[]{:S(2)}) collective-permute-start(f32[128,3,1,128]{3,2,0,1:T(1,128)S(1)} %bitcast.279), channel_id=1, source_target_pairs={{0,1},{2,3},{4,5},{6,7},{8,9},{10,11},{12,13},{14,15},{1,0},{3,2},... | collective-permute-start | bytes 589832 | tf_op jit(solution)/shard_map/ppermute | solution.py:27
  192.6 8.1 %collective-permute-start.16 = (f32[128,3,1,128]{3,2,0,1:T(1,128)S(1)}, f32[128,3,1,128]{3,2,0,1:T(1,128)S(1)}, u32[]{:S(2)}, u32[]{:S(2)}) collective-permute-start(f32[128,3,1,128]{3,2,0,1:T(1,128)S(1)} %get-tuple-element.8), channel_id=1, source_target_pairs={{1,2},{5,6},{7,8},{9,10},{13,14},{2,1},{6,5},{8,7},{10,9},{14,13},... | collective-permute-start | bytes 589832 | tf_op jit(solution)/shard_map/ppermute | solution.py:28
